TPU v7x, 256 devices: a whole 4x4x8 slice. The times are simulated.
256 devices in a mesh: tile: 32 (over x, z), sec: 8 (over y, core).
Axes of the slice: x: 4, y: 4, z: 8, core: 2. Of those that a mesh axis runs over, the one named last changes fastest.
Arguments:
- displacement: float32 [16, 2, 512, 1024], P('sec', None, 'tile'), may hold values from -0.15 to 0.15
- velocity: float32 [16, 2, 512, 1024], P('sec', None, 'tile'), may hold values from -6 to 6
- stiffness: bfloat16 [16, 4, 512, 1024], P('sec', None, 'tile'), may hold values from 0.29882812 to 3
- anchor: float32 [2, 512, 1024], P(None, 'tile'), may hold values from -0.15 to 0.15
- match_source: int32 [16, 8192], P('sec', 'tile'), may hold values from 0 to 16383
- match_target: int32 [16, 8192], P('sec', 'tile'), may hold values from 0 to 16383
- match_weight: float32 [16, 8192], P('sec', 'tile'), may hold values from 1 to 8
- match_count: int32 [16, 32], P('sec', 'tile'), may hold values from 1 to 256, 4096 in all within a row
- reset_mask: int32 [2, 16], P(None, 'sec'), may hold values 0 or 1
Outputs:
- new_displacement: float32 [16, 2, 512, 1024], P('sec', None, 'tile')
- new_velocity: float32 [16, 2, 512, 1024], P('sec', None, 'tile')
Inputs may be any that keep to these rules, and one draw needn't show every extreme that they name: `match_count`: in every section the largest count is 256.
All inputs are finite; a program needn't handle non-finite values. No bound on the sum of `match_count` or of `reset_mask` on one device may be relied on, other than what follows from the above.
Results may differ from a plain program's by a relative error of at most 0.00055.
Values may be sent and summed in bfloat16 or wider, within the bound.
No kernel may reach another device: no remote copies, remote signals or barrier semaphores. Data moves between devices by JAX's collectives and lax.ppermute only.
A program may use at most 128 MiB of HBM per device.

v0:
```python
import jax
import jax.numpy as jnp
from jax import lax
from jax.sharding import PartitionSpec as P

ITERS = 2


max_step = 0.05
time_step = 0.5
mixing = 0.1
epsilon = 1e-06
diagonal_rest = 1.4142135623730951


def from_behind(value, axis, steps):
    count = lax.axis_size(axis)
    leading, last = (max(0, -steps), min(count, count - steps))
    return lax.ppermute(value, axis, [(source, source + steps) for source in range(leading, last)])


def extended(block, sides, width):
    for axis, dim in sides:
        count = lax.axis_size(axis)
        forward = [(i, i + 1) for i in range(count - 1)]
        backward = [(target, source) for source, target in forward]
        low = lax.ppermute(
            lax.slice_in_dim(block, block.shape[dim] - width, None, axis=dim), axis, forward
        )
        high = lax.ppermute(lax.slice_in_dim(block, 0, width, axis=dim), axis, backward)
        block = jnp.concatenate([low, block, high], axis=dim)
    return block


def for_sending(value):

    def short(part):
        return part.astype(jnp.bfloat16) if part.dtype == jnp.float32 else part

    return jax.tree.map(short, value)


def from_left(values):
    return jnp.concatenate([jnp.zeros_like(values[..., :1]), values[..., :-1]], axis=-1)


def from_right(values):
    return jnp.concatenate([values[..., 1:], jnp.zeros_like(values[..., :1])], axis=-1)


def bond_force(first_gap, second_gap, spring_stiff, rest):
    stretch_len = jnp.sqrt(first_gap * first_gap + second_gap * second_gap)
    factor = spring_stiff * (stretch_len - rest) / stretch_len
    return (factor * first_gap, factor * second_gap)


def spring_force(padded, springs, row_start, total_rows):
    band_rows = padded.shape[-2] - 2
    columns = padded.shape[-1]
    stiff_all = springs.astype(jnp.float32)
    bond_rows = row_start - 1 + lax.iota(jnp.int32, band_rows + 1)
    row_valid = ((bond_rows >= 0) & (bond_rows + 1 < total_rows)).astype(jnp.float32)[:, None]
    column_ids = lax.iota(jnp.int32, columns)
    has_right = (column_ids < columns - 1).astype(jnp.float32)
    has_left = (column_ids >= 1).astype(jnp.float32)
    upper_first = padded[..., 0, :-1, :]
    upper_second = padded[..., 1, :-1, :]
    lower_first = padded[..., 0, 1:, :]
    lower_second = padded[..., 1, 1:, :]
    south = bond_force(
        1.0 + lower_first - upper_first,
        lower_second - upper_second,
        stiff_all[..., 1, :, :] * row_valid,
        1.0,
    )
    south_east = bond_force(
        1.0 + from_right(lower_first) - upper_first,
        1.0 + from_right(lower_second) - upper_second,
        stiff_all[..., 2, :, :] * row_valid * has_right,
        diagonal_rest,
    )
    south_west = bond_force(
        1.0 + from_left(lower_first) - upper_first,
        -1.0 + from_left(lower_second) - upper_second,
        stiff_all[..., 3, :, :] * row_valid * has_left,
        diagonal_rest,
    )
    middle_first = padded[..., 0, 1:-1, :]
    middle_second = padded[..., 1, 1:-1, :]
    east = bond_force(
        from_right(middle_first) - middle_first,
        1.0 + from_right(middle_second) - middle_second,
        stiff_all[..., 0, 1:, :] * has_right,
        1.0,
    )

    def summed(part):
        result = south[part][..., 1:, :] - south[part][..., :-1, :]
        result = result + south_east[part][..., 1:, :] - from_left(south_east[part][..., :-1, :])
        result = result + south_west[part][..., 1:, :] - from_right(south_west[part][..., :-1, :])
        return result + east[part] - from_left(east[part])

    return jnp.stack([summed(0), summed(1)], axis=-3)


def pick_nodes(values, index):
    return jax.vmap(lambda field, where: field[:, where])(values, index)


def place_nodes(target, index, amount):
    return jax.vmap(lambda field, where, extra: field.at[:, where].add(extra))(
        target, index, amount
    )


def local(
    displacement,
    velocity,
    stiffness,
    anchor,
    match_source,
    match_target,
    match_weight,
    match_count,
    reset_mask,
):
    sections, _, band_rows, columns = displacement.shape
    slots = match_source.shape[1]
    nodes = band_rows * columns
    band_index = lax.axis_index("tile")
    band_total = lax.axis_size("tile")
    last_group = lax.axis_index("sec") == lax.axis_size("sec") - 1
    upper_stiff = from_behind(stiffness[:, 1:, band_rows - 1 :, :], "tile", 1)
    first_row = jnp.concatenate(
        [jnp.zeros((sections, 1, 1, columns), jnp.bfloat16), upper_stiff], axis=1
    )
    springs = jnp.concatenate([first_row, stiffness], axis=2)
    slot_live = (lax.iota(jnp.int32, slots)[None, :] < match_count).astype(jnp.float32)
    weight_live = match_weight * slot_live
    current = displacement
    speed = velocity
    for iteration in range(ITERS):
        padded = extended(current, (("tile", 2),), 1)
        force = spring_force(padded, springs, band_index * band_rows, band_total * band_rows)
        force = force.reshape(sections, 2, nodes)
        flat = current.reshape(sections, 2, nodes)
        source_points = pick_nodes(flat, match_source)
        next_slab = from_behind(for_sending(current[0]), "sec", -1)
        next_slab = jnp.where(last_group, anchor, next_slab)
        following = jnp.concatenate([flat[1:], next_slab.reshape(1, 2, nodes)], axis=0)
        target_points = pick_nodes(following, match_target)
        match_force = weight_live[:, None, :] * (target_points - source_points)
        force = place_nodes(force, match_source, match_force)
        upper_part = place_nodes(force[1:], match_target[:-1], -match_force[:-1])
        force = jnp.concatenate([force[:1], upper_part], axis=0)
        reaction = place_nodes(
            jnp.zeros((1, 2, nodes), jnp.float32), match_target[-1:], -match_force[-1:]
        )
        returned = from_behind(
            reaction[0].reshape(2, band_rows, columns).astype(jnp.bfloat16), "sec", 1
        ).astype(jnp.float32)
        force = jnp.concatenate([force[:1] + returned.reshape(1, 2, nodes), force[1:]], axis=0)
        force = force.reshape(sections, 2, band_rows, columns)
        velocity_mid = speed + time_step * force
        local_sums = (
            jnp.sum(force * force, axis=(1, 2, 3)),
            jnp.sum(velocity_mid * velocity_mid, axis=(1, 2, 3)),
        )
        force_sq, speed_sq = lax.psum((local_sums[0], local_sums[1]), "tile")
        speed_ratio = jnp.sqrt(speed_sq) / jnp.sqrt(force_sq + epsilon)
        speed = (1.0 - mixing) * velocity_mid + mixing * speed_ratio[:, None, None, None] * force
        keep = (1 - reset_mask[iteration]).astype(jnp.float32)
        speed = speed * keep[:, None, None, None]
        current = current + max_step * jnp.tanh(time_step * speed / max_step)
    return (current, speed)


def solution(mesh):
    placed = (
        P("sec", None, "tile", None),
        P("sec", None, "tile", None),
        P("sec", None, "tile", None),
        P(None, "tile", None),
        P("sec", "tile"),
        P("sec", "tile"),
        P("sec", "tile"),
        P("sec", "tile"),
        P(None, "sec"),
    )
    return jax.shard_map(
        local,
        mesh=mesh,
        in_specs=placed,
        out_specs=(P("sec", None, "tile", None), P("sec", None, "tile", None)),
        check_vma=False,
    )
```

profile of v0, /device:TPU:40, one launch (start us, length us, event | category | flops | bytes accessed | tf_op | source)
XLA Modules:
  0.0 558.0 jit_solution(14257784153946071497)
XLA Ops:
  0.6 0.9 slice.368
  1.6 3.8 collective-permute-start
  5.4 1.0 constant_dynamic-update-slice_fusion
  6.5 2.0 collective-permute-start.1
  8.5 3.8 collective-permute-start.2
  12.3 0.9 fusion.61
  13.2 1.9 collective-permute-start.3
  15.9 0.8 fusion.74
  18.9 9.5 %copy.103 = f32[2,2,16,1024]{1,3,2,0:T(8,128)} copy(f32[2,2,16,1024]{3,2,1,0:T(8,128)} %param.9) | data formatting | bytes 524288 | tf_op args[0]
  28.8 5.5 gather_fusion.1
  36.2 18.4 %stack.25 = f32[2,1,16384]{1,2,0:T(8,128)} reshape(f32[2,16,1024]{2,1,0:T(8,128)S(1)} %get-tuple-element.68) | data formatting | bytes 262144 | tf_op jit(solution)/shard_map/stack | solution.py:103
  54.6 18.4 %stack.24 = f32[2,1,16384]{1,2,0:T(8,128)} reshape(f32[2,16,1024]{2,1,0:T(8,128)S(1)} %get-tuple-element.69) | data formatting | bytes 262144 | tf_op jit(solution)/shard_map/stack | solution.py:103
  73.0 17.3 %pad_maximum_fusion = f32[2,2,16384]{1,2,0:T(8,128)} fusion(f32[2,1,16384]{1,2,0:T(8,128)} %stack.25, f32[2,1,16384]{1,2,0:T(8,128)} %stack.24), kind=kLoop, calls=%fused_computation.10 | loop fusion | flops 65536 | bytes 524288 | tf_op jit(solution)/shard_map/stack | solution.py:103
  90.6 8.3 %copy.102 = f32[2,2,16384]{1,2,0:T(8,128)} copy(f32[2,2,16384]{2,1,0:T(2,128)S(1)} %pad_maximum_fusion.2) | data formatting | bytes 524288 | tf_op jit(solution)/shard_map/concatenate | solution.py:150
  98.9 5.5 gather_fusion
  104.7 5.2 scatter_custom_fusion.1
  109.8 5.1 convert_element_type.96
  114.9 3.7 copy.104
  118.6 2.5 collective-permute-start.4
  121.3 51.5 %scatter_fusion = f32[2,2,16384]{1,2,0:T(8,128)} fusion(f32[2,2,16384]{1,2,0:T(8,128)} %pad_maximum_fusion, s32[512]{0:T(512)S(1)} %bitcast.207, f32[512,2]{1,0:T(8,128)S(1)} %bitcast.228), kind=kCustom, calls=%fused_computation.4 | custom fusion | flops 1024 | bytes 16384 | tf_op jit(solution)/shard_map/vmap()/scatter-add | solution.py:111
  172.8 4.3 copy.105
  177.1 15.1 %slice_add_fusion.1 = (f32[1,2,16384]{1,2,0:T(8,128)}, f32[2,16384]{0,1:T(8,128)}) fusion(f32[2,2,16384]{1,2,0:T(8,128)} %scatter_fusion, f32[2,16,1024]{0,2,1:T(8,128)} %copy.105), kind=kLoop, calls=%fused_computation.15 | loop fusion | flops 32768 | bytes 655360 | tf_op jit(solution)/shard_map/add | solution.py:162
  192.2 8.4 %scatter_custom_fusion.2 = f32[2,16384]{0,1:T(8,128)} fusion(f32[2,16384]{0,1:T(8,128)} %get-tuple-element.23, s32[256]{0:T(256)S(1)} %bitcast.229, f32[2,2,256]{1,2,0:T(8,128)S(1)} %fusion.88), kind=kCustom, calls=%fused_computation.114 | custom fusion | flops 1024 | bytes 262144 | tf_op jit(solution)/shard_map/vmap()/scatter-add | solution.py:111
  200.6 5.4 copy.107
  206.0 5.3 copy.106
  212.0 72.4 %all-reduce.26 = (f32[2]{0:T(128)S(1)}, f32[2]{0:T(128)S(1)}) all-reduce(f32[2]{0:T(128)S(1)} %get-tuple-element.15, f32[2]{0:T(128)S(1)} %multiply_reduce_fusion.3), channel_id=1, replica_groups=mesh['tile'=32,'sec'=8] {'tile'}, use_global_device_ids=true, to_apply=%region_6.7 | all-reduce | flops 4 | bytes 32 | tf_op jit(solution)/shard_map/psum | solution.py:169
  284.7 8.6 %copy.116 = f32[2,2,16,1024]{1,3,2,0:T(8,128)} copy(f32[2,2,16,1024]{3,2,1,0:T(8,128)S(1)} %get-tuple-element.13) | data formatting | bytes 524288 | tf_op jit(solution)/shard_map/add | solution.py:174
  293.5 4.8 collective-permute-start.5
  298.4 1.9 collective-permute-start.6
  300.3 1.9 collective-permute-start.7
  302.5 5.5 gather_fusion.3
  309.4 18.4 %stack.27 = f32[2,1,16384]{1,2,0:T(8,128)} reshape(f32[2,16,1024]{2,1,0:T(8,128)S(1)} %fusion.37) | data formatting | bytes 262144 | tf_op jit(solution)/shard_map/stack | solution.py:103
  328.1 18.4 %stack.26 = f32[2,1,16384]{1,2,0:T(8,128)} reshape(f32[2,16,1024]{2,1,0:T(8,128)S(1)} %fusion.41) | data formatting | bytes 262144 | tf_op jit(solution)/shard_map/stack | solution.py:103
  346.5 17.3 %pad_maximum_fusion.1 = f32[2,2,16384]{1,2,0:T(8,128)} fusion(f32[2,1,16384]{1,2,0:T(8,128)} %stack.27, f32[2,1,16384]{1,2,0:T(8,128)} %stack.26), kind=kLoop, calls=%fused_computation.11 | loop fusion | flops 65536 | bytes 524288 | tf_op jit(solution)/shard_map/stack | solution.py:103
  364.0 8.3 %copy.115 = f32[2,2,16384]{1,2,0:T(8,128)} copy(f32[2,2,16384]{2,1,0:T(2,128)S(1)} %pad_maximum_fusion.4) | data formatting | bytes 524288 | tf_op jit(solution)/shard_map/concatenate | solution.py:150
  372.4 5.5 gather_fusion.2
  378.1 5.2 scatter_custom_fusion.4
  383.2 5.1 convert_element_type.97
  388.4 3.7 copy.117
  392.0 2.6 collective-permute-start.8
  394.7 51.5 %scatter_fusion.1 = f32[2,2,16384]{1,2,0:T(8,128)} fusion(f32[2,2,16384]{1,2,0:T(8,128)} %pad_maximum_fusion.1, s32[512]{0:T(512)S(1)} %bitcast.208, f32[512,2]{1,0:T(8,128)S(1)} %bitcast.227), kind=kCustom, calls=%fused_computation.7 | custom fusion | flops 1024 | bytes 16384 | tf_op jit(solution)/shard_map/vmap()/scatter-add | solution.py:111
  446.3 4.3 copy.118
  450.6 15.1 %slice_add_fusion = (f32[1,2,16384]{1,2,0:T(8,128)}, f32[2,16384]{0,1:T(8,128)}) fusion(f32[2,2,16384]{1,2,0:T(8,128)} %scatter_fusion.1, f32[2,16,1024]{0,2,1:T(8,128)} %copy.118), kind=kLoop, calls=%fused_computation.13 | loop fusion | flops 32768 | bytes 655360 | tf_op jit(solution)/shard_map/add | solution.py:162
  465.7 8.4 %scatter_custom_fusion.5 = f32[2,16384]{0,1:T(8,128)} fusion(f32[2,16384]{0,1:T(8,128)} %get-tuple-element.21, s32[256]{0:T(256)S(1)} %bitcast.230, f32[2,2,256]{1,2,0:T(8,128)S(1)} %fusion.87), kind=kCustom, calls=%fused_computation.92 | custom fusion | flops 1024 | bytes 262144 | tf_op jit(solution)/shard_map/vmap()/scatter-add | solution.py:111
  474.0 5.3 copy.120
  479.4 5.3 copy.119
  485.4 71.6 %all-reduce.25 = (f32[2]{0:T(128)S(1)}, f32[2]{0:T(128)S(1)}) all-reduce(f32[2]{0:T(128)S(1)} %get-tuple-element.8, f32[2]{0:T(128)S(1)} %multiply_reduce_fusion.1), channel_id=1, replica_groups=mesh['tile'=32,'sec'=8] {'tile'}, use_global_device_ids=true, to_apply=%region_13.14 | all-reduce | flops 4 | bytes 32 | tf_op jit(solution)/shard_map/psum | solution.py:169
  557.0 0.9 multiply_add_fusion
  (96 shorter events, 9.8 us)
Async XLA Ops:
  1.6 32.7 %collective-permute-start = (bf16[2,3,1,1024]{3,2,0,1:T(2,128)(2,1)S(1)}, bf16[2,3,1,1024]{3,2,0,1:T(2,128)(2,1)S(1)}, u32[]{:S(2)}, u32[]{:S(2)}) collective-permute-start(bf16[2,3,1,1024]{3,2,0,1:T(2,128)(2,1)S(1)} %copy.130), channel_id=1, source_target_pairs={{0,8},{8,16},{16,24},{24,32},{32,40},{40,48},{48,56},{56,64},{64,7... | collective-permute-start | bytes 36872 | tf_op jit(solution)/shard_map/ppermute | solution.py:19
  6.5 28.1 %collective-permute-start.1 = (f32[2,2,1,1024]{3,2,0,1:T(1,128)S(1)}, f32[2,2,1,1024]{3,2,0,1:T(1,128)S(1)}, u32[]{:S(2)}, u32[]{:S(2)}) collective-permute-start(f32[2,2,1,1024]{3,2,0,1:T(1,128)S(1)} %get-tuple-element.49), channel_id=1, source_target_pairs={{8,0},{16,8},{24,16},{32,24},{40,32},{48,40},{56,48},{64,56},{72,6... | collective-permute-start | bytes 49160 | tf_op jit(solution)/shard_map/ppermute | solution.py:30
  8.5 26.5 %collective-permute-start.2 = (f32[2,2,1,1024]{3,2,0,1:T(1,128)S(1)}, f32[2,2,1,1024]{3,2,0,1:T(1,128)S(1)}, u32[]{:S(2)}, u32[]{:S(2)}) collective-permute-start(f32[2,2,1,1024]{3,2,0,1:T(1,128)S(1)} %get-tuple-element.48), channel_id=1, source_target_pairs={{0,8},{8,16},{16,24},{24,32},{32,40},{40,48},{48,56},{56,64},{64,7... | collective-permute-start | bytes 49160 | tf_op jit(solution)/shard_map/ppermute | solution.py:27
  13.2 77.1 %collective-permute-start.3 = (bf16[2,16,1024]{2,1,0:T(8,128)(2,1)S(1)}, bf16[2,16,1024]{2,1,0:T(8,128)(2,1)S(1)}, u32[]{:S(2)}, u32[]{:S(2)}) collective-permute-start(bf16[2,16,1024]{2,1,0:T(8,128)(2,1)S(1)} %fusion.61), channel_id=1, source_target_pairs={{1,0},{2,1},{3,2},{4,3},{5,4},{6,5},{7,6},{9,8},{10,9},{11,10},{12... | collective-permute-start | bytes 196616 | tf_op jit(solution)/shard_map/ppermute | solution.py:19
  18.9 9.7 %slice-start = ((f32[2,2,16,1024]{3,2,1,0:T(8,128)}), f32[1,2,16,1024]{3,2,1,0:T(8,128)S(1)}, s32[]{:S(2)}) async-start(f32[2,2,16,1024]{3,2,1,0:T(8,128)} %param.9), calls=%async_computation | async-start | bytes 262144 | tf_op jit(solution)/shard_map/slice | solution.py:150
  18.9 15.4 %copy-start.3 = (bf16[2,4,16,1024]{3,2,1,0:T(8,128)(2,1)S(1)}, bf16[2,4,16,1024]{3,2,1,0:T(8,128)(2,1)}, u32[]{:S(2)}) copy-start(bf16[2,4,16,1024]{3,2,1,0:T(8,128)(2,1)} %param.11) | copy-start | bytes 786436
  73.0 17.3 %copy-start.2 = (f32[2,16,1024]{2,1,0:T(8,128)S(1)}, f32[2,16,1024]{2,1,0:T(8,128)}, u32[]{:S(2)}) copy-start(f32[2,16,1024]{2,1,0:T(8,128)} %param.12) | copy-start | bytes 393220
  118.6 54.2 %collective-permute-start.4 = (bf16[2,16,1024]{2,1,0:T(8,128)(2,1)S(1)}, bf16[2,16,1024]{2,1,0:T(8,128)(2,1)S(1)}, u32[]{:S(2)}, u32[]{:S(2)}) collective-permute-start(bf16[2,16,1024]{2,1,0:T(8,128)(2,1)S(1)} %copy.104), channel_id=1, source_target_pairs={{0,1},{1,2},{2,3},{3,4},{4,5},{5,6},{6,7},{8,9},{9,10},{10,11},{11... | collective-permute-start | bytes 196616 | tf_op jit(solution)/shard_map/ppermute | solution.py:19
  200.6 11.3 %copy-start.1 = (f32[2,2,16,1024]{3,2,1,0:T(8,128)S(1)}, f32[2,2,16,1024]{3,2,1,0:T(8,128)}, u32[]{:S(2)}) copy-start(f32[2,2,16,1024]{3,2,1,0:T(8,128)} %param.10) | copy-start | bytes 786436
  200.6 83.9 %copy-start = (f32[2,2,16,1024]{3,2,1,0:T(8,128)S(1)}, f32[2,2,16,1024]{3,2,1,0:T(8,128)}, u32[]{:S(2)}) copy-start(f32[2,2,16,1024]{3,2,1,0:T(8,128)} %param.9) | copy-start | bytes 786436
  293.5 14.5 %collective-permute-start.5 = (f32[2,2,1,1024]{3,2,0,1:T(1,128)S(1)}, f32[2,2,1,1024]{3,2,0,1:T(1,128)S(1)}, u32[]{:S(2)}, u32[]{:S(2)}) collective-permute-start(f32[2,2,1,1024]{3,2,0,1:T(1,128)S(1)} %get-tuple-element.45), channel_id=1, source_target_pairs={{8,0},{16,8},{24,16},{32,24},{40,32},{48,40},{56,48},{64,56},{72,6... | collective-permute-start | bytes 49160 | tf_op jit(solution)/shard_map/ppermute | solution.py:30
  298.4 10.1 %collective-permute-start.6 = (f32[2,2,1,1024]{3,2,0,1:T(1,128)S(1)}, f32[2,2,1,1024]{3,2,0,1:T(1,128)S(1)}, u32[]{:S(2)}, u32[]{:S(2)}) collective-permute-start(f32[2,2,1,1024]{3,2,0,1:T(1,128)S(1)} %get-tuple-element.44), channel_id=1, source_target_pairs={{0,8},{8,16},{16,24},{24,32},{32,40},{40,48},{48,56},{56,64},{64,7... | collective-permute-start | bytes 49160 | tf_op jit(solution)/shard_map/ppermute | solution.py:27
  300.3 63.5 %collective-permute-start.7 = (bf16[2,16,1024]{2,1,0:T(8,128)(2,1)S(1)}, bf16[2,16,1024]{2,1,0:T(8,128)(2,1)S(1)}, u32[]{:S(2)}, u32[]{:S(2)}) collective-permute-start(bf16[2,16,1024]{2,1,0:T(8,128)(2,1)S(1)} %fusion.62), channel_id=1, source_target_pairs={{1,0},{2,1},{3,2},{4,3},{5,4},{6,5},{7,6},{9,8},{10,9},{11,10},{12... | collective-permute-start | bytes 196616 | tf_op jit(solution)/shard_map/ppermute | solution.py:19
  392.0 54.2 %collective-permute-start.8 = (bf16[2,16,1024]{2,1,0:T(8,128)(2,1)S(1)}, bf16[2,16,1024]{2,1,0:T(8,128)(2,1)S(1)}, u32[]{:S(2)}, u32[]{:S(2)}) collective-permute-start(bf16[2,16,1024]{2,1,0:T(8,128)(2,1)S(1)} %copy.117), channel_id=1, source_target_pairs={{0,1},{1,2},{2,3},{3,4},{4,5},{5,6},{6,7},{8,9},{9,10},{10,11},{11... | collective-permute-start | bytes 196616 | tf_op jit(solution)/shard_map/ppermute | solution.py:19
where the time goes:
time: 562 us; the launch traced here: 558 us
  other arithmetic  214 us (38%)
  local copies, waits for them, and re-layouts  173 us (31%)
  blocking collectives  144 us (26%)
  starting transfers between devices  25.3 us (5%)
    psum x2, blocking collectives, local(): force_sq, speed_sq = lax.psum((local_sums[0], local_sums[1]), 'tile')  144 us
    scatter-add x8, other arithmetic, place_nodes(): field.at[:, where].add(extra)  130 us
    another operation x4, local copies, waits for them, and re-layouts, spring_force(): return jnp.stack([summed(0), summed(1)], axis=-3)  73.7 us
    another operation x2, other arithmetic, spring_force(): return jnp.stack([summed(0), summed(1)], axis=-3)  34.5 us
    add x2, other arithmetic, local(): force[:1] + returned.reshape(1, 2, nodes)  30.1 us
    gather x4, local copies, waits for them, and re-layouts, pick_nodes(): return jax.vmap(lambda field, where: field[:, where])(values, index)  22.1 us
    concatenate x2, local copies, waits for them, and re-layouts, local(): jnp.concatenate([flat[1:], next_slab.reshape(1, 2, nodes)], axis=0)  16.7 us
    ppermute x5, starting transfers between devices, from_behind(): lax.ppermute(value, axis, [(source, source + steps) for source in range(l...  12.8 us
  transfers between devices with their start and end apart: 9, of which 0 were waited for; matrix products, arithmetic and copies ran while one was open for 43% of the time, Pallas kernels for 0%

commit v1 on v0

v1 whole, which is shorter than its diff:
```python
import jax
import jax.numpy as jnp
from jax import lax
from jax.experimental import pallas as pl
from jax.experimental.pallas import tpu as pltpu
from jax.sharding import PartitionSpec as P

ITERS = 2


max_step = 0.05
time_step = 0.5
mixing = 0.1
epsilon = 1e-06
diagonal_rest = 1.4142135623730951
HIGHEST = lax.Precision.HIGHEST


def shifted(value, axis, steps):
    count = lax.axis_size(axis)
    pairs = [(i, i + steps) for i in range(count) if 0 <= i + steps < count]
    return lax.ppermute(value, axis, pairs)


def tile_sum(value):
    count = lax.axis_size("tile")
    if count & (count - 1):
        return lax.psum(value, "tile")
    step = 1
    while step < count:
        value = value + lax.ppermute(value, "tile", [(i, i ^ step) for i in range(count)])
        step *= 2
    return value


def bond(first_gap, second_gap, spring_stiff, rest):
    stretch_len = jnp.sqrt(first_gap * first_gap + second_gap * second_gap)
    factor = spring_stiff * (stretch_len - rest) / stretch_len
    return (factor * first_gap, factor * second_gap)


def spring_kernel(u_ref, top_ref, bot_ref, k_ref, kt_ref, keep_ref, out_ref):
    sections, _, rows, columns = u_ref.shape
    row = lax.broadcasted_iota(jnp.int32, (rows, columns), 0)
    col = lax.broadcasted_iota(jnp.int32, (rows, columns), 1)
    col_one = lax.broadcasted_iota(jnp.int32, (1, columns), 1)
    keep_top = keep_ref[0:1, :]
    keep_bot = keep_ref[1:2, :]
    last_row = row == rows - 1
    down_keep = jnp.where(last_row, keep_bot, 1.0)

    def east_of(x):
        return pltpu.roll(x, columns - 1, 1)

    def west_of(x):
        return pltpu.roll(x, 1, 1)

    for s in range(sections):
        x0 = u_ref[s, 0]
        x1 = u_ref[s, 1]
        t0 = top_ref[s, 0]
        t1 = top_ref[s, 1]
        l0 = jnp.where(last_row, bot_ref[s, 0], pltpu.roll(x0, rows - 1, 0))
        l1 = jnp.where(last_row, bot_ref[s, 1], pltpu.roll(x1, rows - 1, 0))
        k_east = jnp.where(col < columns - 1, k_ref[s, 0].astype(jnp.float32), 0.0)
        k_south = k_ref[s, 1].astype(jnp.float32) * down_keep
        k_se = jnp.where(col < columns - 1, k_ref[s, 2].astype(jnp.float32) * down_keep, 0.0)
        k_sw = jnp.where(col >= 1, k_ref[s, 3].astype(jnp.float32) * down_keep, 0.0)
        south = bond(1.0 + l0 - x0, l1 - x1, k_south, 1.0)
        south_east = bond(
            1.0 + east_of(l0) - x0, 1.0 + east_of(l1) - x1, k_se, diagonal_rest
        )
        south_west = bond(
            1.0 + west_of(l0) - x0, -1.0 + west_of(l1) - x1, k_sw, diagonal_rest
        )
        east = bond(east_of(x0) - x0, 1.0 + east_of(x1) - x1, k_east, 1.0)
        r0 = x0[0:1, :]
        r1 = x1[0:1, :]
        kt_south = kt_ref[s, 0].astype(jnp.float32) * keep_top
        kt_se = jnp.where(col_one < columns - 1, kt_ref[s, 1].astype(jnp.float32) * keep_top, 0.0)
        kt_sw = jnp.where(col_one >= 1, kt_ref[s, 2].astype(jnp.float32) * keep_top, 0.0)
        top_south = bond(1.0 + r0 - t0, r1 - t1, kt_south, 1.0)
        top_se = bond(1.0 + east_of(r0) - t0, 1.0 + east_of(r1) - t1, kt_se, diagonal_rest)
        top_sw = bond(1.0 + west_of(r0) - t0, -1.0 + west_of(r1) - t1, kt_sw, diagonal_rest)
        for part in range(2):
            below = south[part] + west_of(south_east[part]) + east_of(south_west[part])
            below_top = top_south[part] + west_of(top_se[part]) + east_of(top_sw[part])
            incoming = jnp.where(row == 0, below_top, pltpu.roll(below, 1, 0))
            owned = south[part] + south_east[part] + south_west[part] + east[part]
            out_ref[s, part] = owned - incoming - west_of(east[part])


def spring_force(current, top, bottom, stiffness, top_stiff, keep):
    return pl.pallas_call(
        spring_kernel,
        out_shape=jax.ShapeDtypeStruct(current.shape, jnp.float32),
    )(current, top, bottom, stiffness, top_stiff, keep)


def one_hots(index, band_rows, columns):
    row = index // columns
    col = index % columns
    col_hot = (col[..., None] == lax.iota(jnp.int32, columns)).astype(jnp.float32)
    row_hot = (row[..., :, None] == lax.iota(jnp.int32, band_rows)).astype(jnp.float32)
    return col_hot, jnp.swapaxes(row_hot, -1, -2)


def gather_points(field, col_hot, row_hot):
    picked = jnp.einsum("scrk,sjk->scrj", field, col_hot, precision=HIGHEST)
    return jnp.sum(picked * row_hot[:, None], axis=2)


def scatter_points(values, col_hot, row_hot):
    spread = values[:, :, None, :] * row_hot[:, None]
    return jnp.einsum("scrj,sjk->scrk", spread, col_hot, precision=HIGHEST)


def local(
    displacement,
    velocity,
    stiffness,
    anchor,
    match_source,
    match_target,
    match_weight,
    match_count,
    reset_mask,
):
    sections, _, band_rows, columns = displacement.shape
    slots = match_source.shape[1]
    band_index = lax.axis_index("tile")
    band_total = lax.axis_size("tile")
    last_group = lax.axis_index("sec") == lax.axis_size("sec") - 1
    top_stiff = shifted(stiffness[:, 1:, band_rows - 1 :, :], "tile", 1)
    keep = jnp.stack(
        [
            jnp.where(band_index > 0, 1.0, 0.0),
            jnp.where(band_index < band_total - 1, 1.0, 0.0),
        ]
        + [jnp.float32(0.0)] * 6
    ).astype(jnp.float32)
    keep = jnp.broadcast_to(keep[:, None], (8, columns))
    slot_live = (lax.iota(jnp.int32, slots)[None, :] < match_count).astype(jnp.float32)
    weight_live = match_weight * slot_live
    target_prev = shifted(match_target[-1], "sec", 1)
    weight_prev = shifted(weight_live[-1], "sec", 1)
    gather_index = jnp.stack(
        [
            jnp.concatenate([match_source[0], target_prev]),
            jnp.concatenate([match_source[1], match_target[0]]),
        ]
    )
    col_hot, row_hot = one_hots(gather_index, band_rows, columns)
    anchor_hot = one_hots(match_target[-1:], band_rows, columns)
    anchor_points = gather_points(anchor[None], *anchor_hot)[0]
    current = displacement
    speed = velocity
    for iteration in range(ITERS):
        top = shifted(current[:, :, band_rows - 1 :, :], "tile", 1)
        bottom = shifted(current[:, :, :1, :], "tile", -1)
        points = gather_points(current, col_hot, row_hot)
        source_first = points[0, :, :slots]
        target_back = points[0, :, slots:]
        source_last = points[1, :, :slots]
        target_first = points[1, :, slots:]
        source_prev = shifted(source_last, "sec", 1)
        target_last = shifted(target_back, "sec", -1)
        target_last = jnp.where(last_group, anchor_points, target_last)
        force_first = weight_live[0] * (target_first - source_first)
        force_last = weight_live[1] * (target_last - source_last)
        force_prev = weight_prev * (target_back - source_prev)
        values = jnp.stack(
            [
                jnp.concatenate([force_first, -force_prev], axis=-1),
                jnp.concatenate([force_last, -force_first], axis=-1),
            ]
        )
        matched = scatter_points(values, col_hot, row_hot)
        force = spring_force(current, top, bottom, stiffness, top_stiff, keep) + matched
        velocity_mid = speed + time_step * force
        sums = tile_sum(
            jnp.stack(
                [
                    jnp.sum(force * force, axis=(1, 2, 3)),
                    jnp.sum(velocity_mid * velocity_mid, axis=(1, 2, 3)),
                ]
            )
        )
        force_sq, speed_sq = sums[0], sums[1]
        speed_ratio = jnp.sqrt(speed_sq) / jnp.sqrt(force_sq + epsilon)
        speed = (1.0 - mixing) * velocity_mid + mixing * speed_ratio[:, None, None, None] * force
        keep_speed = (1 - reset_mask[iteration]).astype(jnp.float32)
        speed = speed * keep_speed[:, None, None, None]
        current = current + max_step * jnp.tanh(time_step * speed / max_step)
    return (current, speed)


def solution(mesh):
    placed = (
        P("sec", None, "tile", None),
        P("sec", None, "tile", None),
        P("sec", None, "tile", None),
        P(None, "tile", None),
        P("sec", "tile"),
        P("sec", "tile"),
        P("sec", "tile"),
        P("sec", "tile"),
        P(None, "sec"),
    )
    return jax.shard_map(
        local,
        mesh=mesh,
        in_specs=placed,
        out_specs=(P("sec", None, "tile", None), P("sec", None, "tile", None)),
        check_vma=False,
    )
```

time: 562 us -> 117 us (0.21)
  the two profiles are of different devices: /device:TPU:40 before, /device:TPU:14 now
where the time goes in v1:
time: 117 us; the launch traced here: 116 us
  waiting for transfers between devices  51.1 us (44%)
  starting transfers between devices  40.7 us (35%)
  matrix products  8.37 us (7%)
  other arithmetic  5.97 us (5%)
  Pallas kernels  5.17 us (4%)
  local copies, waits for them, and re-layouts  4.06 us (3%)
    ppermute x10, waiting for transfers between devices, tile_sum(): lax.ppermute(value, 'tile', [(i, i ^ step) for i in range(count)])  42.8 us
    ppermute x11, starting transfers between devices, shifted(): return lax.ppermute(value, axis, pairs)  34.5 us
    ppermute x11, waiting for transfers between devices, shifted(): return lax.ppermute(value, axis, pairs)  8.29 us
    ppermute x10, starting transfers between devices, tile_sum(): lax.ppermute(value, 'tile', [(i, i ^ step) for i in range(count)])  6.19 us
    pallas_call x2, Pallas kernels, spring_force(): pl.pallas_call(spring_kernel, out_shape=jax.ShapeDtypeStruct(current.shap...  5.17 us
    dot_general x3, matrix products, gather_points(): picked = jnp.einsum('scrk,sjk->scrj', field, col_hot, precision=HIGHEST)  5.11 us
    dot_general x2, matrix products, scatter_points(): return jnp.einsum('scrj,sjk->scrk', spread, col_hot, precision=HIGHEST)  3.26 us
  transfers between devices with their start and end apart: 21, of which 12 were waited for; matrix products, arithmetic and copies ran while one was open for 9% of the time, Pallas kernels for 0%

profile of v1, /device:TPU:14, one launch (start us, length us, event | category | flops | bytes accessed | tf_op | source)
XLA Modules:
  0.0 116.5 jit_solution(12464637588667683625)
XLA Ops:
  0.6 0.8 and_select_fusion.2
  1.4 1.9 %collective-permute-start.3 = (s32[256]{0:T(256)S(1)}, s32[256]{0:T(256)S(1)}, u32[]{:S(2)}, u32[]{:S(2)}) collective-permute-start(s32[256]{0:T(256)S(1)} %bitcast.123), channel_id=1, source_target_pairs={{0,1},{1,2},{2,3},{3,4},{4,5},{5,6},{6,7},{8,9},{9,10},{10,11},{11... | collective-permute-start | bytes 3080 | tf_op jit(solution)/shard_map/ppermute | solution.py:22
  3.3 0.8 compare_select_fusion
  4.1 3.6 %collective-permute-start.4 = (f32[256]{0:T(256)S(1)}, f32[256]{0:T(256)S(1)}, u32[]{:S(2)}, u32[]{:S(2)}) collective-permute-start(f32[256]{0:T(256)S(1)} %bitcast.99), channel_id=1, source_target_pairs={{0,1},{1,2},{2,3},{3,4},{4,5},{5,6},{6,7},{8,9},{9,10},{10,11},{11... | collective-permute-start | bytes 3080 | tf_op jit(solution)/shard_map/ppermute | solution.py:22
  7.7 1.0 fusion.51
  8.7 8.2 %collective-permute-start.1 = (f32[2,2,1,1024]{3,2,1,0:T(1,128)S(1)}, f32[2,2,1,1024]{3,2,1,0:T(1,128)S(1)}, u32[]{:S(2)}, u32[]{:S(2)}) collective-permute-start(f32[2,2,1,1024]{3,2,1,0:T(1,128)S(1)} %get-tuple-element.20), channel_id=1, source_target_pairs={{8,0},{16,8},{24,16},{32,24},{40,32},{48,40},{56,48},{64,56},{72,6... | collective-permute-start | bytes 49160 | tf_op jit(solution)/shard_map/ppermute | solution.py:22
  16.9 1.9 %collective-permute-start = (f32[2,2,1,1024]{3,2,1,0:T(1,128)S(1)}, f32[2,2,1,1024]{3,2,1,0:T(1,128)S(1)}, u32[]{:S(2)}, u32[]{:S(2)}) collective-permute-start(f32[2,2,1,1024]{3,2,1,0:T(1,128)S(1)} %get-tuple-element.21), channel_id=1, source_target_pairs={{0,8},{8,16},{16,24},{24,32},{32,40},{40,48},{48,56},{56,64},{64,7... | collective-permute-start | bytes 49160 | tf_op jit(solution)/shard_map/ppermute | solution.py:22
  18.8 0.8 convert_bitcast_fusion.1
  19.6 0.8 fusion.53
  20.4 0.7 fusion.29
  21.2 2.2 %fusion.25 = f32[2,2,512]{2,1,0:T(2,128)S(1)} fusion(f32[2,2,16,1024]{3,2,1,0:T(8,128)S(1)} %copy-done.3, s32[2,512]{1,0:T(2,128)S(1)} %get-tuple-element.35, f32[2,16,512]{2,1,0:T(8,128)S(1)} %fusion.39), kind=kOutput, calls=%fused_computation.14 | convolution fusion | flops 403765248 | bytes 339968 | tf_op jit(solution)/shard_map/scrk,sjk->scrj/dot_general | solution.py:109
  23.4 1.9 %collective-permute-start.5 = (f32[2,256]{1,0:T(2,128)S(1)}, f32[2,256]{1,0:T(2,128)S(1)}, u32[]{:S(2)}, u32[]{:S(2)}) collective-permute-start(f32[2,256]{1,0:T(2,128)S(1)} %get-tuple-element.32), channel_id=1, source_target_pairs={{0,1},{1,2},{2,3},{3,4},{4,5},{5,6},{6,7},{8,9},{9,10},{10,11},{11... | collective-permute-start | bytes 6152 | tf_op jit(solution)/shard_map/ppermute | solution.py:22
  25.3 3.6 %collective-permute-start.6 = (f32[2,256]{1,0:T(2,128)S(1)}, f32[2,256]{1,0:T(2,128)S(1)}, u32[]{:S(2)}, u32[]{:S(2)}) collective-permute-start(f32[2,256]{1,0:T(2,128)S(1)} %get-tuple-element.33), channel_id=1, source_target_pairs={{1,0},{2,1},{3,2},{4,3},{5,4},{6,5},{7,6},{9,8},{10,9},{11,10},{12... | collective-permute-start | bytes 6152 | tf_op jit(solution)/shard_map/ppermute | solution.py:22
  29.1 0.9 slice.81
  30.0 1.9 %collective-permute-start.2 = (bf16[2,3,1,1024]{3,2,1,0:T(2,128)(2,1)S(1)}, bf16[2,3,1,1024]{3,2,1,0:T(2,128)(2,1)S(1)}, u32[]{:S(2)}, u32[]{:S(2)}) collective-permute-start(bf16[2,3,1,1024]{3,2,1,0:T(2,128)(2,1)S(1)} %slice.81), channel_id=1, source_target_pairs={{0,8},{8,16},{16,24},{24,32},{32,40},{40,48},{48,56},{56,64},{64,7... | collective-permute-start | bytes 36872 | tf_op jit(solution)/shard_map/ppermute | solution.py:22
  32.0 1.6 %fusion.5 = f32[2,2,16,1024]{3,2,1,0:T(8,128)S(1)} fusion(s32[2,512]{1,0:T(2,128)S(1)} %get-tuple-element.35, f32[2,2,512]{2,1,0:T(2,128)S(1)} %pad_maximum_fusion, f32[2,16,512]{2,1,0:T(8,128)S(1)} %fusion.39), kind=kOutput, calls=%fused_computation.4 | convolution fusion | flops 403734528 | bytes 339968 | tf_op jit(solution)/shard_map/scrj,sjk->scrk/dot_general | solution.py:115
  33.6 4.2 %collective-permute-done.2.kt_ref = bf16[2,3,1,1024]{3,2,1,0:T(2,128)(2,1)S(1)} collective-permute-done((bf16[2,3,1,1024]{3,2,1,0:T(2,128)(2,1)S(1)}, bf16[2,3,1,1024]{3,2,1,0:T(2,128)(2,1)S(1)}, u32[]{:S(2)}, u32[]{:S(2)}) %collective-permute-start.2) | collective-permute-done | bytes 12320 | tf_op jit(solution)/shard_map/ppermute | solution.py:22
  37.9 0.7 broadcast_in_dim.2.keep_ref
  38.6 2.6 %shard_map.104 = f32[2,2,16,1024]{3,2,1,0:T(8,128)} custom-call(f32[2,2,16,1024]{3,2,1,0:T(8,128)} %u_ref.1, f32[2,2,1,1024]{3,2,1,0:T(1,128)} %copy-done.8, f32[2,2,1,1024]{3,2,1,0:T(1,128)} %copy-done.7, bf16[2,4,16,1024]{3,2,1,0:T(8,128)(2,1)} %k_ref.3, bf16[2,3,1,1024]{3,2,1,0:T(2,128)(2,1)} %copy-done.6, f32[8,1024]{1,0:T(8,128)} %broadcast_in_dim.2.keep_ref), custom_call_target="tpu_custom_call" | custom-call | tf_op jit(solution)/shard_map/pallas_call | solution.py:94
  41.2 1.2 multiply_reduce_fusion.3
  42.4 3.6 %collective-permute-done.7 = f32[2,2]{1,0:T(2,128)S(1)} collective-permute-done((f32[2,2]{1,0:T(2,128)S(1)}, f32[2,2]{1,0:T(2,128)S(1)}, u32[]{:S(2)}, u32[]{:S(2)}) %collective-permute-start.7) | collective-permute-done | bytes 48 | tf_op jit(solution)/shard_map/ppermute | solution.py:31
  46.1 4.5 %collective-permute-done.8 = f32[2,2]{1,0:T(2,128)S(1)} collective-permute-done((f32[2,2]{1,0:T(2,128)S(1)}, f32[2,2]{1,0:T(2,128)S(1)}, u32[]{:S(2)}, u32[]{:S(2)}) %collective-permute-start.8) | collective-permute-done | bytes 48 | tf_op jit(solution)/shard_map/ppermute | solution.py:31
  50.6 2.3 %collective-permute-start.9 = (f32[2,2]{1,0:T(2,128)S(1)}, f32[2,2]{1,0:T(2,128)S(1)}, u32[]{:S(2)}, u32[]{:S(2)}) collective-permute-start(f32[2,2]{1,0:T(2,128)S(1)} %fusion.58), channel_id=1, source_target_pairs={{0,32},{8,40},{16,48},{24,56},{32,0},{40,8},{48,16},{56,24},{64,96... | collective-permute-start | bytes 56 | tf_op jit(solution)/shard_map/ppermute | solution.py:31
  52.9 5.3 %collective-permute-done.9 = f32[2,2]{1,0:T(2,128)S(1)} collective-permute-done((f32[2,2]{1,0:T(2,128)S(1)}, f32[2,2]{1,0:T(2,128)S(1)}, u32[]{:S(2)}, u32[]{:S(2)}) %collective-permute-start.9) | collective-permute-done | bytes 48 | tf_op jit(solution)/shard_map/ppermute | solution.py:31
  58.2 0.5 collective-permute-start.10
  58.7 3.0 %collective-permute-done.10 = f32[2,2]{1,0:T(2,128)S(1)} collective-permute-done((f32[2,2]{1,0:T(2,128)S(1)}, f32[2,2]{1,0:T(2,128)S(1)}, u32[]{:S(2)}, u32[]{:S(2)}) %collective-permute-start.10) | collective-permute-done | bytes 48 | tf_op jit(solution)/shard_map/ppermute | solution.py:31
  61.7 1.1 collective-permute-start.11
  62.9 4.0 %collective-permute-done.11 = f32[2,2]{1,0:T(2,128)S(1)} collective-permute-done((f32[2,2]{1,0:T(2,128)S(1)}, f32[2,2]{1,0:T(2,128)S(1)}, u32[]{:S(2)}, u32[]{:S(2)}) %collective-permute-start.11) | collective-permute-done | bytes 48 | tf_op jit(solution)/shard_map/ppermute | solution.py:31
  66.8 0.1 multiply_add_fusion.2
  67.0 2.2 %fusion.22 = f32[2,2,512]{2,1,0:T(2,128)S(1)} fusion(f32[2,2,16,1024]{3,2,1,0:T(8,128)S(1)} %get-tuple-element.11.u_ref, s32[2,512]{1,0:T(2,128)S(1)} %get-tuple-element.35, f32[2,16,512]{2,1,0:T(8,128)S(1)} %fusion.39), kind=kOutput, calls=%fused_computation.13 | convolution fusion | flops 403765248 | bytes 339968 | tf_op jit(solution)/shard_map/scrk,sjk->scrj/dot_general | solution.py:109
  69.2 1.9 %collective-permute-start.14 = (f32[2,256]{1,0:T(2,128)S(1)}, f32[2,256]{1,0:T(2,128)S(1)}, u32[]{:S(2)}, u32[]{:S(2)}) collective-permute-start(f32[2,256]{1,0:T(2,128)S(1)} %get-tuple-element.26), channel_id=1, source_target_pairs={{0,1},{1,2},{2,3},{3,4},{4,5},{5,6},{6,7},{8,9},{9,10},{10,11},{11... | collective-permute-start | bytes 6152 | tf_op jit(solution)/shard_map/ppermute | solution.py:22
  71.2 3.6 %collective-permute-start.15 = (f32[2,256]{1,0:T(2,128)S(1)}, f32[2,256]{1,0:T(2,128)S(1)}, u32[]{:S(2)}, u32[]{:S(2)}) collective-permute-start(f32[2,256]{1,0:T(2,128)S(1)} %get-tuple-element.27), channel_id=1, source_target_pairs={{1,0},{2,1},{3,2},{4,3},{5,4},{6,5},{7,6},{9,8},{10,9},{11,10},{12... | collective-permute-start | bytes 6152 | tf_op jit(solution)/shard_map/ppermute | solution.py:22
  74.8 3.9 %collective-permute-start.13 = (f32[2,2,1,1024]{3,2,1,0:T(1,128)S(1)}, f32[2,2,1,1024]{3,2,1,0:T(1,128)S(1)}, u32[]{:S(2)}, u32[]{:S(2)}) collective-permute-start(f32[2,2,1,1024]{3,2,1,0:T(1,128)S(1)} %get-tuple-element.18), channel_id=1, source_target_pairs={{8,0},{16,8},{24,16},{32,24},{40,32},{48,40},{56,48},{64,56},{72,6... | collective-permute-start | bytes 49160 | tf_op jit(solution)/shard_map/ppermute | solution.py:22
  78.8 1.9 %collective-permute-start.12 = (f32[2,2,1,1024]{3,2,1,0:T(1,128)S(1)}, f32[2,2,1,1024]{3,2,1,0:T(1,128)S(1)}, u32[]{:S(2)}, u32[]{:S(2)}) collective-permute-start(f32[2,2,1,1024]{3,2,1,0:T(1,128)S(1)} %get-tuple-element.19), channel_id=1, source_target_pairs={{0,8},{8,16},{16,24},{24,32},{32,40},{40,48},{48,56},{56,64},{64,7... | collective-permute-start | bytes 49160 | tf_op jit(solution)/shard_map/ppermute | solution.py:22
  80.8 1.6 %fusion.1 = f32[2,2,16,1024]{3,2,1,0:T(8,128)S(1)} fusion(s32[2,512]{1,0:T(2,128)S(1)} %get-tuple-element.35, f32[2,2,512]{2,1,0:T(2,128)S(1)} %pad_maximum_fusion.1, f32[2,16,512]{2,1,0:T(8,128)S(1)} %fusion.39), kind=kOutput, calls=%fused_computation.2 | convolution fusion | flops 403734528 | bytes 339968 | tf_op jit(solution)/shard_map/scrj,sjk->scrk/dot_general | solution.py:115
  82.4 4.1 %collective-permute-done.12.top_ref = f32[2,2,1,1024]{3,2,1,0:T(1,128)S(1)} collective-permute-done((f32[2,2,1,1024]{3,2,1,0:T(1,128)S(1)}, f32[2,2,1,1024]{3,2,1,0:T(1,128)S(1)}, u32[]{:S(2)}, u32[]{:S(2)}) %collective-permute-start.12) | collective-permute-done | bytes 16416 | tf_op jit(solution)/shard_map/ppermute | solution.py:22
  86.5 0.6 copy-done.10
  87.1 2.6 %shard_map.105 = f32[2,2,16,1024]{3,2,1,0:T(8,128)} custom-call(f32[2,2,16,1024]{3,2,1,0:T(8,128)} %copy-done.1, f32[2,2,1,1024]{3,2,1,0:T(1,128)} %copy-done.10, f32[2,2,1,1024]{3,2,1,0:T(1,128)} %copy-done.9, bf16[2,4,16,1024]{3,2,1,0:T(8,128)(2,1)} %k_ref.3, bf16[2,3,1,1024]{3,2,1,0:T(2,128)(2,1)} %copy-done.6, f32[8,1024]{1,0:T(8,128)} %broadcast_in_dim.2.keep_ref), custom_call_target="tpu_custom_call" | custom-call | tf_op jit(solution)/shard_map/pallas_call | solution.py:94
  89.7 1.2 multiply_reduce_fusion.1
  90.9 0.3 collective-permute-start.16
  91.1 3.6 %collective-permute-done.16 = f32[2,2]{1,0:T(2,128)S(1)} collective-permute-done((f32[2,2]{1,0:T(2,128)S(1)}, f32[2,2]{1,0:T(2,128)S(1)}, u32[]{:S(2)}, u32[]{:S(2)}) %collective-permute-start.16) | collective-permute-done | bytes 48 | tf_op jit(solution)/shard_map/ppermute | solution.py:31
  94.8 4.5 %collective-permute-done.17 = f32[2,2]{1,0:T(2,128)S(1)} collective-permute-done((f32[2,2]{1,0:T(2,128)S(1)}, f32[2,2]{1,0:T(2,128)S(1)}, u32[]{:S(2)}, u32[]{:S(2)}) %collective-permute-start.17) | collective-permute-done | bytes 48 | tf_op jit(solution)/shard_map/ppermute | solution.py:31
  99.4 7.5 %collective-permute-done.18 = f32[2,2]{1,0:T(2,128)S(1)} collective-permute-done((f32[2,2]{1,0:T(2,128)S(1)}, f32[2,2]{1,0:T(2,128)S(1)}, u32[]{:S(2)}, u32[]{:S(2)}) %collective-permute-start.18) | collective-permute-done | bytes 48 | tf_op jit(solution)/shard_map/ppermute | solution.py:31
  106.8 0.5 collective-permute-start.19
  107.4 3.0 %collective-permute-done.19 = f32[2,2]{1,0:T(2,128)S(1)} collective-permute-done((f32[2,2]{1,0:T(2,128)S(1)}, f32[2,2]{1,0:T(2,128)S(1)}, u32[]{:S(2)}, u32[]{:S(2)}) %collective-permute-start.19) | collective-permute-done | bytes 48 | tf_op jit(solution)/shard_map/ppermute | solution.py:31
  110.4 1.1 collective-permute-start.20
  111.5 4.0 %collective-permute-done.20 = f32[2,2]{1,0:T(2,128)S(1)} collective-permute-done((f32[2,2]{1,0:T(2,128)S(1)}, f32[2,2]{1,0:T(2,128)S(1)}, u32[]{:S(2)}, u32[]{:S(2)}) %collective-permute-start.20) | collective-permute-done | bytes 48 | tf_op jit(solution)/shard_map/ppermute | solution.py:31
  115.5 0.9 multiply_add_fusion
  (68 shorter events, 0.8 us)
Async XLA Ops:
  0.6 19.7 %copy-start = (f32[2,16,1024]{2,1,0:T(8,128)S(1)}, f32[2,16,1024]{2,1,0:T(8,128)}, u32[]{:S(2)}) copy-start(f32[2,16,1024]{2,1,0:T(8,128)} %param.12) | copy-start | bytes 393220
  1.4 19.7 %collective-permute-start.3 = (s32[256]{0:T(256)S(1)}, s32[256]{0:T(256)S(1)}, u32[]{:S(2)}, u32[]{:S(2)}) collective-permute-start(s32[256]{0:T(256)S(1)} %bitcast.123), channel_id=1, source_target_pairs={{0,1},{1,2},{2,3},{3,4},{4,5},{5,6},{6,7},{8,9},{9,10},{10,11},{11... | collective-permute-start | bytes 3080 | tf_op jit(solution)/shard_map/ppermute | solution.py:22
  4.1 25.9 %collective-permute-start.4 = (f32[256]{0:T(256)S(1)}, f32[256]{0:T(256)S(1)}, u32[]{:S(2)}, u32[]{:S(2)}) collective-permute-start(f32[256]{0:T(256)S(1)} %bitcast.99), channel_id=1, source_target_pairs={{0,1},{1,2},{2,3},{3,4},{4,5},{5,6},{6,7},{8,9},{9,10},{10,11},{11... | collective-permute-start | bytes 3080 | tf_op jit(solution)/shard_map/ppermute | solution.py:22
  8.7 12.5 %copy-start.3 = (f32[2,2,16,1024]{3,2,1,0:T(8,128)S(1)}, f32[2,2,16,1024]{3,2,1,0:T(8,128)}, u32[]{:S(2)}) copy-start(f32[2,2,16,1024]{3,2,1,0:T(8,128)} %u_ref.1) | copy-start | bytes 786436
  8.7 29.1 %collective-permute-start.1 = (f32[2,2,1,1024]{3,2,1,0:T(1,128)S(1)}, f32[2,2,1,1024]{3,2,1,0:T(1,128)S(1)}, u32[]{:S(2)}, u32[]{:S(2)}) collective-permute-start(f32[2,2,1,1024]{3,2,1,0:T(1,128)S(1)} %get-tuple-element.20), channel_id=1, source_target_pairs={{8,0},{16,8},{24,16},{32,24},{40,32},{48,40},{56,48},{64,56},{72,6... | collective-permute-start | bytes 49160 | tf_op jit(solution)/shard_map/ppermute | solution.py:22
  16.9 21.0 %collective-permute-start = (f32[2,2,1,1024]{3,2,1,0:T(1,128)S(1)}, f32[2,2,1,1024]{3,2,1,0:T(1,128)S(1)}, u32[]{:S(2)}, u32[]{:S(2)}) collective-permute-start(f32[2,2,1,1024]{3,2,1,0:T(1,128)S(1)} %get-tuple-element.21), channel_id=1, source_target_pairs={{0,8},{8,16},{16,24},{24,32},{32,40},{40,48},{48,56},{56,64},{64,7... | collective-permute-start | bytes 49160 | tf_op jit(solution)/shard_map/ppermute | solution.py:22
  23.4 8.6 %collective-permute-start.5 = (f32[2,256]{1,0:T(2,128)S(1)}, f32[2,256]{1,0:T(2,128)S(1)}, u32[]{:S(2)}, u32[]{:S(2)}) collective-permute-start(f32[2,256]{1,0:T(2,128)S(1)} %get-tuple-element.32), channel_id=1, source_target_pairs={{0,1},{1,2},{2,3},{3,4},{4,5},{5,6},{6,7},{8,9},{9,10},{10,11},{11... | collective-permute-start | bytes 6152 | tf_op jit(solution)/shard_map/ppermute | solution.py:22
  25.3 6.6 %collective-permute-start.6 = (f32[2,256]{1,0:T(2,128)S(1)}, f32[2,256]{1,0:T(2,128)S(1)}, u32[]{:S(2)}, u32[]{:S(2)}) collective-permute-start(f32[2,256]{1,0:T(2,128)S(1)} %get-tuple-element.33), channel_id=1, source_target_pairs={{1,0},{2,1},{3,2},{4,3},{5,4},{6,5},{7,6},{9,8},{10,9},{11,10},{12... | collective-permute-start | bytes 6152 | tf_op jit(solution)/shard_map/ppermute | solution.py:22
  30.0 7.8 %collective-permute-start.2 = (bf16[2,3,1,1024]{3,2,1,0:T(2,128)(2,1)S(1)}, bf16[2,3,1,1024]{3,2,1,0:T(2,128)(2,1)S(1)}, u32[]{:S(2)}, u32[]{:S(2)}) collective-permute-start(bf16[2,3,1,1024]{3,2,1,0:T(2,128)(2,1)S(1)} %slice.81), channel_id=1, source_target_pairs={{0,8},{8,16},{16,24},{24,32},{32,40},{40,48},{48,56},{56,64},{64,7... | collective-permute-start | bytes 36872 | tf_op jit(solution)/shard_map/ppermute | solution.py:22
  37.8 0.7 copy-start.6
  37.8 0.7 copy-start.7
  37.9 0.7 copy-start.8
  38.6 2.6 %copy-start.5 = (f32[2,2,16,1024]{3,2,1,0:T(8,128)S(1)}, f32[2,2,16,1024]{3,2,1,0:T(8,128)}, u32[]{:S(2)}) copy-start(f32[2,2,16,1024]{3,2,1,0:T(8,128)} %param.10) | copy-start | bytes 786436
  41.2 25.7 %copy-start.4 = (f32[2,2,16,1024]{3,2,1,0:T(8,128)S(1)}, f32[2,2,16,1024]{3,2,1,0:T(8,128)}, u32[]{:S(2)}) copy-start(f32[2,2,16,1024]{3,2,1,0:T(8,128)} %u_ref.1) | copy-start | bytes 786436
  42.3 3.7 %collective-permute-start.7 = (f32[2,2]{1,0:T(2,128)S(1)}, f32[2,2]{1,0:T(2,128)S(1)}, u32[]{:S(2)}, u32[]{:S(2)}) collective-permute-start(f32[2,2]{1,0:T(2,128)S(1)} %pad_maximum_fusion.2), channel_id=1, source_target_pairs={{0,8},{8,0},{16,24},{24,16},{32,40},{40,32},{48,56},{56,48},{64,72... | collective-permute-start | bytes 56 | tf_op jit(solution)/shard_map/ppermute | solution.py:31
  46.0 4.6 %collective-permute-start.8 = (f32[2,2]{1,0:T(2,128)S(1)}, f32[2,2]{1,0:T(2,128)S(1)}, u32[]{:S(2)}, u32[]{:S(2)}) collective-permute-start(f32[2,2]{1,0:T(2,128)S(1)} %fusion.45), channel_id=1, source_target_pairs={{0,16},{8,24},{16,0},{24,8},{32,48},{40,56},{48,32},{56,40},{64,80... | collective-permute-start | bytes 56 | tf_op jit(solution)/shard_map/ppermute | solution.py:31
  50.6 7.6 %collective-permute-start.9 = (f32[2,2]{1,0:T(2,128)S(1)}, f32[2,2]{1,0:T(2,128)S(1)}, u32[]{:S(2)}, u32[]{:S(2)}) collective-permute-start(f32[2,2]{1,0:T(2,128)S(1)} %fusion.58), channel_id=1, source_target_pairs={{0,32},{8,40},{16,48},{24,56},{32,0},{40,8},{48,16},{56,24},{64,96... | collective-permute-start | bytes 56 | tf_op jit(solution)/shard_map/ppermute | solution.py:31
  58.2 3.6 %collective-permute-start.10 = (f32[2,2]{1,0:T(2,128)S(1)}, f32[2,2]{1,0:T(2,128)S(1)}, u32[]{:S(2)}, u32[]{:S(2)}) collective-permute-start(f32[2,2]{1,0:T(2,128)S(1)} %add.98), channel_id=1, source_target_pairs={{0,64},{8,72},{16,80},{24,88},{32,96},{40,104},{48,112},{56,120},{... | collective-permute-start | bytes 56 | tf_op jit(solution)/shard_map/ppermute | solution.py:31
  61.7 5.1 %collective-permute-start.11 = (f32[2,2]{1,0:T(2,128)S(1)}, f32[2,2]{1,0:T(2,128)S(1)}, u32[]{:S(2)}, u32[]{:S(2)}) collective-permute-start(f32[2,2]{1,0:T(2,128)S(1)} %add.99), channel_id=1, source_target_pairs={{0,128},{8,136},{16,144},{24,152},{32,160},{40,168},{48,176},{56,1... | collective-permute-start | bytes 56 | tf_op jit(solution)/shard_map/ppermute | solution.py:31
  67.0 7.8 %copy-start.1 = (f32[2,2,16,1024]{3,2,1,0:T(8,128)}, f32[2,2,16,1024]{3,2,1,0:T(8,128)S(1)}, u32[]{:S(2)}) copy-start(f32[2,2,16,1024]{3,2,1,0:T(8,128)S(1)} %get-tuple-element.11.u_ref) | copy-start | bytes 786436
  69.2 11.5 %collective-permute-start.14 = (f32[2,256]{1,0:T(2,128)S(1)}, f32[2,256]{1,0:T(2,128)S(1)}, u32[]{:S(2)}, u32[]{:S(2)}) collective-permute-start(f32[2,256]{1,0:T(2,128)S(1)} %get-tuple-element.26), channel_id=1, source_target_pairs={{0,1},{1,2},{2,3},{3,4},{4,5},{5,6},{6,7},{8,9},{9,10},{10,11},{11... | collective-permute-start | bytes 6152 | tf_op jit(solution)/shard_map/ppermute | solution.py:22
  71.2 9.6 %collective-permute-start.15 = (f32[2,256]{1,0:T(2,128)S(1)}, f32[2,256]{1,0:T(2,128)S(1)}, u32[]{:S(2)}, u32[]{:S(2)}) collective-permute-start(f32[2,256]{1,0:T(2,128)S(1)} %get-tuple-element.27), channel_id=1, source_target_pairs={{1,0},{2,1},{3,2},{4,3},{5,4},{6,5},{7,6},{9,8},{10,9},{11,10},{12... | collective-permute-start | bytes 6152 | tf_op jit(solution)/shard_map/ppermute | solution.py:22
  74.8 7.6 %collective-permute-start.13 = (f32[2,2,1,1024]{3,2,1,0:T(1,128)S(1)}, f32[2,2,1,1024]{3,2,1,0:T(1,128)S(1)}, u32[]{:S(2)}, u32[]{:S(2)}) collective-permute-start(f32[2,2,1,1024]{3,2,1,0:T(1,128)S(1)} %get-tuple-element.18), channel_id=1, source_target_pairs={{8,0},{16,8},{24,16},{32,24},{40,32},{48,40},{56,48},{64,56},{72,6... | collective-permute-start | bytes 49160 | tf_op jit(solution)/shard_map/ppermute | solution.py:22
  78.8 7.7 %collective-permute-start.12 = (f32[2,2,1,1024]{3,2,1,0:T(1,128)S(1)}, f32[2,2,1,1024]{3,2,1,0:T(1,128)S(1)}, u32[]{:S(2)}, u32[]{:S(2)}) collective-permute-start(f32[2,2,1,1024]{3,2,1,0:T(1,128)S(1)} %get-tuple-element.19), channel_id=1, source_target_pairs={{0,8},{8,16},{16,24},{24,32},{32,40},{40,48},{48,56},{56,64},{64,7... | collective-permute-start | bytes 49160 | tf_op jit(solution)/shard_map/ppermute | solution.py:22
  82.4 4.1 %copy-start.9 = (f32[2,2,1,1024]{3,2,1,0:T(1,128)}, f32[2,2,1,1024]{3,2,1,0:T(1,128)S(1)}, u32[]{:S(2)}) copy-start(f32[2,2,1,1024]{3,2,1,0:T(1,128)S(1)} %collective-permute-done.13.bot_ref) | copy-start | bytes 49156
  86.5 0.6 copy-start.10
  89.7 25.8 %copy-start.2 = (f32[2,2,16,1024]{3,2,1,0:T(8,128)S(1)}, f32[2,2,16,1024]{3,2,1,0:T(8,128)}, u32[]{:S(2)}) copy-start(f32[2,2,16,1024]{3,2,1,0:T(8,128)} %copy-done.1) | copy-start | bytes 786436
  90.9 3.8 %collective-permute-start.16 = (f32[2,2]{1,0:T(2,128)S(1)}, f32[2,2]{1,0:T(2,128)S(1)}, u32[]{:S(2)}, u32[]{:S(2)}) collective-permute-start(f32[2,2]{1,0:T(2,128)S(1)} %pad_maximum_fusion.3), channel_id=1, source_target_pairs={{0,8},{8,0},{16,24},{24,16},{32,40},{40,32},{48,56},{56,48},{64,72... | collective-permute-start | bytes 56 | tf_op jit(solution)/shard_map/ppermute | solution.py:31
  94.7 4.6 %collective-permute-start.17 = (f32[2,2]{1,0:T(2,128)S(1)}, f32[2,2]{1,0:T(2,128)S(1)}, u32[]{:S(2)}, u32[]{:S(2)}) collective-permute-start(f32[2,2]{1,0:T(2,128)S(1)} %fusion.44), channel_id=1, source_target_pairs={{0,16},{8,24},{16,0},{24,8},{32,48},{40,56},{48,32},{56,40},{64,80... | collective-permute-start | bytes 56 | tf_op jit(solution)/shard_map/ppermute | solution.py:31
  99.3 7.6 %collective-permute-start.18 = (f32[2,2]{1,0:T(2,128)S(1)}, f32[2,2]{1,0:T(2,128)S(1)}, u32[]{:S(2)}, u32[]{:S(2)}) collective-permute-start(f32[2,2]{1,0:T(2,128)S(1)} %fusion.57), channel_id=1, source_target_pairs={{0,32},{8,40},{16,48},{24,56},{32,0},{40,8},{48,16},{56,24},{64,96... | collective-permute-start | bytes 56 | tf_op jit(solution)/shard_map/ppermute | solution.py:31
  106.8 3.6 %collective-permute-start.19 = (f32[2,2]{1,0:T(2,128)S(1)}, f32[2,2]{1,0:T(2,128)S(1)}, u32[]{:S(2)}, u32[]{:S(2)}) collective-permute-start(f32[2,2]{1,0:T(2,128)S(1)} %add.108), channel_id=1, source_target_pairs={{0,64},{8,72},{16,80},{24,88},{32,96},{40,104},{48,112},{56,120},{... | collective-permute-start | bytes 56 | tf_op jit(solution)/shard_map/ppermute | solution.py:31
  110.4 5.1 %collective-permute-start.20 = (f32[2,2]{1,0:T(2,128)S(1)}, f32[2,2]{1,0:T(2,128)S(1)}, u32[]{:S(2)}, u32[]{:S(2)}) collective-permute-start(f32[2,2]{1,0:T(2,128)S(1)} %add.109), channel_id=1, source_target_pairs={{0,128},{8,136},{16,144},{24,152},{32,160},{40,168},{48,176},{56,1... | collective-permute-start | bytes 56 | tf_op jit(solution)/shard_map/ppermute | solution.py:31

commit v2 on v1

--- a/solution.py
+++ b/solution.py
@@ -39,7 +39,7 @@
     return (factor * first_gap, factor * second_gap)
 
 
-def spring_kernel(u_ref, top_ref, bot_ref, k_ref, kt_ref, keep_ref, out_ref):
+def spring_kernel(u_ref, top_ref, bot_ref, k_ref, keep_ref, out_ref):
     sections, _, rows, columns = u_ref.shape
     row = lax.broadcasted_iota(jnp.int32, (rows, columns), 0)
     col = lax.broadcasted_iota(jnp.int32, (rows, columns), 1)
@@ -76,9 +76,9 @@
         east = bond(east_of(x0) - x0, 1.0 + east_of(x1) - x1, k_east, 1.0)
         r0 = x0[0:1, :]
         r1 = x1[0:1, :]
-        kt_south = kt_ref[s, 0].astype(jnp.float32) * keep_top
-        kt_se = jnp.where(col_one < columns - 1, kt_ref[s, 1].astype(jnp.float32) * keep_top, 0.0)
-        kt_sw = jnp.where(col_one >= 1, kt_ref[s, 2].astype(jnp.float32) * keep_top, 0.0)
+        kt_south = top_ref[s, 2] * keep_top
+        kt_se = jnp.where(col_one < columns - 1, top_ref[s, 3] * keep_top, 0.0)
+        kt_sw = jnp.where(col_one >= 1, top_ref[s, 4] * keep_top, 0.0)
         top_south = bond(1.0 + r0 - t0, r1 - t1, kt_south, 1.0)
         top_se = bond(1.0 + east_of(r0) - t0, 1.0 + east_of(r1) - t1, kt_se, diagonal_rest)
         top_sw = bond(1.0 + west_of(r0) - t0, -1.0 + west_of(r1) - t1, kt_sw, diagonal_rest)
@@ -90,29 +90,37 @@
             out_ref[s, part] = owned - incoming - west_of(east[part])
 
 
-def spring_force(current, top, bottom, stiffness, top_stiff, keep):
+def spring_force(current, top, bottom, stiffness, keep):
     return pl.pallas_call(
         spring_kernel,
         out_shape=jax.ShapeDtypeStruct(current.shape, jnp.float32),
-    )(current, top, bottom, stiffness, top_stiff, keep)
+    )(current, top, bottom, stiffness, keep)
 
 
 def one_hots(index, band_rows, columns):
     row = index // columns
     col = index % columns
-    col_hot = (col[..., None] == lax.iota(jnp.int32, columns)).astype(jnp.float32)
-    row_hot = (row[..., :, None] == lax.iota(jnp.int32, band_rows)).astype(jnp.float32)
-    return col_hot, jnp.swapaxes(row_hot, -1, -2)
-
-
-def gather_points(field, col_hot, row_hot):
-    picked = jnp.einsum("scrk,sjk->scrj", field, col_hot, precision=HIGHEST)
-    return jnp.sum(picked * row_hot[:, None], axis=2)
-
-
-def scatter_points(values, col_hot, row_hot):
-    spread = values[:, :, None, :] * row_hot[:, None]
-    return jnp.einsum("scrj,sjk->scrk", spread, col_hot, precision=HIGHEST)
+    col_hot = (col[:, None] == lax.iota(jnp.int32, columns)[None, :]).astype(jnp.float32)
+    row_hot = (lax.iota(jnp.int32, band_rows)[:, None] == row[None, :]).astype(jnp.float32)
+    return col_hot, row_hot
+
+
+def gather_points(field, hots):
+    col_hot, row_hot = hots
+    picked = jnp.einsum("crk,jk->crj", field, col_hot, precision=HIGHEST)
+    return jnp.sum(picked * row_hot[None], axis=1)
+
+
+def scatter_points(values, hots):
+    col_hot, row_hot = hots
+    spread = values[:, None, :] * row_hot[None]
+    return jnp.einsum("crj,jk->crk", spread, col_hot, precision=HIGHEST)
+
+
+def advanced(current, velocity_mid, force, speed_ratio, keep_speed):
+    speed = (1.0 - mixing) * velocity_mid + mixing * speed_ratio * force
+    speed = speed * keep_speed
+    return current + max_step * jnp.tanh(time_step * speed / max_step), speed
 
 
 def local(
@@ -131,7 +139,6 @@
     band_index = lax.axis_index("tile")
     band_total = lax.axis_size("tile")
     last_group = lax.axis_index("sec") == lax.axis_size("sec") - 1
-    top_stiff = shifted(stiffness[:, 1:, band_rows - 1 :, :], "tile", 1)
     keep = jnp.stack(
         [
             jnp.where(band_index > 0, 1.0, 0.0),
@@ -142,56 +149,87 @@
     keep = jnp.broadcast_to(keep[:, None], (8, columns))
     slot_live = (lax.iota(jnp.int32, slots)[None, :] < match_count).astype(jnp.float32)
     weight_live = match_weight * slot_live
-    target_prev = shifted(match_target[-1], "sec", 1)
-    weight_prev = shifted(weight_live[-1], "sec", 1)
-    gather_index = jnp.stack(
-        [
-            jnp.concatenate([match_source[0], target_prev]),
-            jnp.concatenate([match_source[1], match_target[0]]),
-        ]
-    )
-    col_hot, row_hot = one_hots(gather_index, band_rows, columns)
-    anchor_hot = one_hots(match_target[-1:], band_rows, columns)
-    anchor_points = gather_points(anchor[None], *anchor_hot)[0]
+    hots_last = one_hots(jnp.concatenate([match_source[1], match_target[0]]), band_rows, columns)
+    points_last = gather_points(displacement[1], hots_last)
+    forward = shifted(
+        jnp.concatenate(
+            [
+                points_last[:, :slots],
+                match_target[1][None].astype(jnp.float32),
+                weight_live[1][None],
+            ]
+        ),
+        "sec",
+        1,
+    )
+    source_prev = forward[:2]
+    target_prev = forward[2].astype(jnp.int32)
+    weight_prev = forward[3]
+    hots_first = one_hots(jnp.concatenate([match_source[0], target_prev]), band_rows, columns)
+    points_first = gather_points(displacement[0], hots_first)
+    anchor_points = gather_points(anchor, one_hots(match_target[1], band_rows, columns))
+    top_stiff = stiffness[:, 1:, band_rows - 1 :, :].astype(jnp.float32)
+    first_top = shifted(
+        jnp.concatenate([displacement[:, :, band_rows - 1 :, :], top_stiff], axis=1), "tile", 1
+    )
+    top_stiff = first_top[:, 2:]
+    top = first_top[:, :2]
+    bottom = shifted(displacement[:, :, :1, :], "tile", -1)
     current = displacement
     speed = velocity
     for iteration in range(ITERS):
-        top = shifted(current[:, :, band_rows - 1 :, :], "tile", 1)
-        bottom = shifted(current[:, :, :1, :], "tile", -1)
-        points = gather_points(current, col_hot, row_hot)
-        source_first = points[0, :, :slots]
-        target_back = points[0, :, slots:]
-        source_last = points[1, :, :slots]
-        target_first = points[1, :, slots:]
-        source_prev = shifted(source_last, "sec", 1)
+        source_first = points_first[:, :slots]
+        target_back = points_first[:, slots:]
+        source_last = points_last[:, :slots]
+        target_first = points_last[:, slots:]
+        if iteration > 0:
+            source_prev = shifted(source_last, "sec", 1)
         target_last = shifted(target_back, "sec", -1)
         target_last = jnp.where(last_group, anchor_points, target_last)
+        spring = spring_force(
+            current, jnp.concatenate([top, top_stiff], axis=1), bottom, stiffness, keep
+        )
         force_first = weight_live[0] * (target_first - source_first)
         force_last = weight_live[1] * (target_last - source_last)
         force_prev = weight_prev * (target_back - source_prev)
-        values = jnp.stack(
+        matched = jnp.stack(
             [
-                jnp.concatenate([force_first, -force_prev], axis=-1),
-                jnp.concatenate([force_last, -force_first], axis=-1),
+                scatter_points(jnp.concatenate([force_first, -force_prev], axis=-1), hots_first),
+                scatter_points(jnp.concatenate([force_last, -force_first], axis=-1), hots_last),
             ]
         )
-        matched = scatter_points(values, col_hot, row_hot)
-        force = spring_force(current, top, bottom, stiffness, top_stiff, keep) + matched
+        force = spring + matched
         velocity_mid = speed + time_step * force
-        sums = tile_sum(
-            jnp.stack(
-                [
-                    jnp.sum(force * force, axis=(1, 2, 3)),
-                    jnp.sum(velocity_mid * velocity_mid, axis=(1, 2, 3)),
-                ]
-            )
-        )
+        local_sums = jnp.stack(
+            [
+                jnp.sum(force * force, axis=(1, 2, 3)),
+                jnp.sum(velocity_mid * velocity_mid, axis=(1, 2, 3)),
+            ]
+        )
+        if iteration + 1 < ITERS:
+            parts = jnp.concatenate([current, velocity_mid, force], axis=1)
+            parts_first = gather_points(parts[0], hots_first)
+            parts_last = gather_points(parts[1], hots_last)
+            top_parts = shifted(parts[:, :, band_rows - 1 :, :], "tile", 1)
+            bottom_parts = shifted(parts[:, :, :1, :], "tile", -1)
+        sums = tile_sum(local_sums)
         force_sq, speed_sq = sums[0], sums[1]
         speed_ratio = jnp.sqrt(speed_sq) / jnp.sqrt(force_sq + epsilon)
-        speed = (1.0 - mixing) * velocity_mid + mixing * speed_ratio[:, None, None, None] * force
         keep_speed = (1 - reset_mask[iteration]).astype(jnp.float32)
-        speed = speed * keep_speed[:, None, None, None]
-        current = current + max_step * jnp.tanh(time_step * speed / max_step)
+        ratio4 = speed_ratio[:, None, None, None]
+        keep4 = keep_speed[:, None, None, None]
+        current, speed = advanced(current, velocity_mid, force, ratio4, keep4)
+        if iteration + 1 < ITERS:
+
+            def moved(stacked, ratio, keep_one):
+                return advanced(stacked[:2], stacked[2:4], stacked[4:], ratio, keep_one)[0]
+
+            points_first = moved(parts_first, speed_ratio[0], keep_speed[0])
+            points_last = moved(parts_last, speed_ratio[1], keep_speed[1])
+            top = moved(jnp.swapaxes(top_parts, 0, 1), ratio4[:, 0], keep4[:, 0])
+            top = jnp.swapaxes(top, 0, 1)
+            bottom = moved(jnp.swapaxes(bottom_parts, 0, 1), ratio4[:, 0], keep4[:, 0])
+            bottom = jnp.swapaxes(bottom, 0, 1)
     return (current, speed)
 
 

time: 117 us -> 106 us (0.906)
  waiting for transfers between devices: 51.1 us -> 37.2 us
  other arithmetic: 5.97 us -> 9.84 us
  starting transfers between devices: 40.7 us -> 37.7 us
  matrix products: 8.37 us -> 10.2 us
  local copies, waits for them, and re-layouts: 4.06 us -> 2.75 us
  between operations: 1.12 us -> 2.31 us
    ppermute x10, waiting for transfers between devices: 42.8 us -> 35.1 us  [tile_sum(): lax.ppermute(value, 'tile', [(i, i ^ step) for i in range(count)])]
    ppermute x11 -> x8, starting transfers between devices: 34.5 us -> 27.5 us  [shifted(): return lax.ppermute(value, axis, pairs)]
    ppermute x11 -> x8, waiting for transfers between devices: 8.29 us -> 2.04 us  [shifted(): return lax.ppermute(value, axis, pairs)]
    ppermute x10, starting transfers between devices: 6.19 us -> 10.2 us  [tile_sum(): lax.ppermute(value, 'tile', [(i, i ^ step) for i in range(count)])]
    add x2 -> x4, other arithmetic: 1.07 us -> 3.05 us  [advanced(): return (current + max_step * jnp.tanh(time_step * speed / max_step), speed)]
    dot_general x5 -> x9, matrix products: 8.37 us -> 10.2 us  [the longest x5 6.59 us: gather_points(): picked = jnp.einsum('crk,jk->crj', field, col_hot, precision=HIGHEST)]
  transfers between devices with their start and end apart: 21 -> 18, of which waited for: 12 -> 12; matrix products, arithmetic and copies ran while one was open for 9% -> 10% of each run, Pallas kernels for 0% -> 0%
where the time goes in v2:
time: 106 us; the launch traced here: 105 us
  starting transfers between devices  37.7 us (36%)
  waiting for transfers between devices  37.2 us (35%)
  matrix products  10.2 us (10%)
  other arithmetic  9.84 us (9%)
  Pallas kernels  5.23 us (5%)
  local copies, waits for them, and re-layouts  2.75 us (3%)
  between operations  2.31 us (2%)
    ppermute x10, waiting for transfers between devices, tile_sum(): lax.ppermute(value, 'tile', [(i, i ^ step) for i in range(count)])  35.1 us
    ppermute x8, starting transfers between devices, shifted(): return lax.ppermute(value, axis, pairs)  27.5 us
    ppermute x10, starting transfers between devices, tile_sum(): lax.ppermute(value, 'tile', [(i, i ^ step) for i in range(count)])  10.2 us
    dot_general x5, matrix products, gather_points(): picked = jnp.einsum('crk,jk->crj', field, col_hot, precision=HIGHEST)  6.59 us
    pallas_call x2, Pallas kernels, spring_force(): pl.pallas_call(spring_kernel, out_shape=jax.ShapeDtypeStruct(current.shap...  5.23 us
    dot_general x4, matrix products, scatter_points(): return jnp.einsum('crj,jk->crk', spread, col_hot, precision=HIGHEST)  3.61 us
    add x4, other arithmetic, advanced(): return (current + max_step * jnp.tanh(time_step * speed / max_step), speed)  3.05 us
    reduce_sum x2, other arithmetic, local(): jnp.sum(force * force, axis=(1, 2, 3))  2.31 us
  transfers between devices with their start and end apart: 18, of which 12 were waited for; matrix products, arithmetic and copies ran while one was open for 10% of the time, Pallas kernels for 0%

profile of v2, /device:TPU:14, one launch (start us, length us, event | category | flops | bytes accessed | tf_op | source)
XLA Modules:
  0.0 105.1 jit_solution(5013943035183809489)
XLA Ops:
  0.7 0.8 and_select_fusion
  1.4 0.8 fusion.119
  2.2 2.1 %fusion.57 = f32[2,512]{1,0:T(2,128)S(1)} fusion(s32[512]{0:T(512)S(1)} %get-tuple-element.43, f32[2,2,16,1024]{3,2,1,0:T(8,128)} %u_ref.1, f32[16,512]{1,0:T(8,128)S(1)} %fusion.89), kind=kOutput, calls=%fused_computation.25 | convolution fusion | flops 201882624 | bytes 169984 | tf_op jit(solution)/shard_map/crk,jk->crj/dot_general | solution.py:110
  4.4 0.8 compare_select_fusion
  5.1 1.9 %collective-permute-start.2 = (f32[4,256]{1,0:T(4,128)S(1)}, f32[4,256]{1,0:T(4,128)S(1)}, u32[]{:S(2)}, u32[]{:S(2)}) collective-permute-start(f32[4,256]{1,0:T(4,128)S(1)} %pad_maximum_fusion.5), channel_id=1, source_target_pairs={{0,1},{1,2},{2,3},{3,4},{4,5},{5,6},{6,7},{8,9},{9,10},{10,11},{11... | collective-permute-start | bytes 12296 | tf_op jit(solution)/shard_map/ppermute | solution.py:22
  7.1 0.9 slice_convert_fusion
  8.1 3.8 %collective-permute-start = (f32[2,5,1,1024]{3,2,1,0:T(1,128)S(1)}, f32[2,5,1,1024]{3,2,1,0:T(1,128)S(1)}, u32[]{:S(2)}, u32[]{:S(2)}) collective-permute-start(f32[2,5,1,1024]{3,2,1,0:T(1,128)S(1)} %pad_maximum_fusion.3), channel_id=1, source_target_pairs={{0,8},{8,16},{16,24},{24,32},{32,40},{40,48},{48,56},{56,64},{64,7... | collective-permute-start | bytes 122888 | tf_op jit(solution)/shard_map/ppermute | solution.py:22
  11.9 6.1 %collective-permute-start.1 = (f32[2,2,1,1024]{3,2,1,0:T(1,128)S(1)}, f32[2,2,1,1024]{3,2,1,0:T(1,128)S(1)}, u32[]{:S(2)}, u32[]{:S(2)}) collective-permute-start(f32[2,2,1,1024]{3,2,1,0:T(1,128)S(1)} %get-tuple-element.20), channel_id=1, source_target_pairs={{8,0},{16,8},{24,16},{32,24},{40,32},{48,40},{56,48},{64,56},{72,6... | collective-permute-start | bytes 49160 | tf_op jit(solution)/shard_map/ppermute | solution.py:22
  18.1 0.6 fusion.121
  18.7 0.7 fusion.61
  19.6 1.2 %fusion.54 = f32[2,512]{1,0:T(2,128)S(1)} fusion(s32[512]{0:T(512)S(1)} %get-tuple-element.39, f32[2,2,16,1024]{3,2,1,0:T(8,128)S(1)} %copy-done.1, f32[16,512]{1,0:T(8,128)S(1)} %fusion.90), kind=kOutput, calls=%fused_computation.24 | convolution fusion | flops 201882624 | bytes 169984 | tf_op jit(solution)/shard_map/crk,jk->crj/dot_general | solution.py:110
  20.8 3.4 %collective-permute-start.3 = (f32[2,256]{1,0:T(2,128)S(1)}, f32[2,256]{1,0:T(2,128)S(1)}, u32[]{:S(2)}, u32[]{:S(2)}) collective-permute-start(f32[2,256]{1,0:T(2,128)S(1)} %get-tuple-element.27), channel_id=1, source_target_pairs={{1,0},{2,1},{3,2},{4,3},{5,4},{6,5},{7,6},{9,8},{10,9},{11,10},{12... | collective-permute-start | bytes 6152 | tf_op jit(solution)/shard_map/ppermute | solution.py:22
  24.2 0.9 fusion.24
  25.5 0.9 fusion.30
  26.4 0.7 broadcast_in_dim.2.keep_ref
  27.1 2.6 %shard_map.104 = f32[2,2,16,1024]{3,2,1,0:T(8,128)} custom-call(f32[2,2,16,1024]{3,2,1,0:T(8,128)} %u_ref.1, f32[2,5,1,1024]{3,2,1,0:T(1,128)} %copy-done.6, f32[2,2,1,1024]{3,2,1,0:T(1,128)} %copy-done.7, bf16[2,4,16,1024]{3,2,1,0:T(8,128)(2,1)} %k_ref.3, f32[8,1024]{1,0:T(8,128)} %broadcast_in_dim.2.keep_ref), custom_call_target="tpu_custom_call" | custom-call | tf_op jit(solution)/shard_map/pallas_call | solution.py:94
  29.7 1.1 %multiply_reduce_fusion.3 = (f32[2]{0:T(128)S(1)}, f32[2,2,16,1024]{3,2,1,0:T(8,128)S(1)}) fusion(f32[2,2,16,1024]{3,2,1,0:T(8,128)} %shard_map.104, f32[1,2,16,1024]{3,2,1,0:T(8,128)S(1)} %fusion.30, f32[1,2,16,1024]{3,2,1,0:T(8,128)S(1)} %fusion.24), kind=kLoop, calls=%fused_computation.53 | loop fusion | flops 262142 | bytes 786440 | tf_op jit(solution)/shard_map/reduce_sum | solution.py:205
  31.1 1.3 %fusion.39 = f32[6,512]{1,0:T(8,128)S(1)} fusion(s32[512]{0:T(512)S(1)} %get-tuple-element.39, f32[2,6,16,1024]{3,2,1,0:T(8,128)S(1)} %pad_maximum_fusion, f32[16,512]{1,0:T(8,128)S(1)} %fusion.90), kind=kOutput, calls=%fused_computation.19 | convolution fusion | flops 604599296 | bytes 440320 | tf_op jit(solution)/shard_map/crk,jk->crj/dot_general | solution.py:110
  32.4 1.3 %fusion.36 = f32[6,512]{1,0:T(8,128)S(1)} fusion(s32[512]{0:T(512)S(1)} %get-tuple-element.43, f32[2,6,16,1024]{3,2,1,0:T(8,128)S(1)} %pad_maximum_fusion, f32[16,512]{1,0:T(8,128)S(1)} %fusion.89), kind=kOutput, calls=%fused_computation.18 | convolution fusion | flops 604599296 | bytes 440320 | tf_op jit(solution)/shard_map/crk,jk->crj/dot_general | solution.py:110
  33.9 3.9 %collective-permute-start.9 = (f32[2,6,1,1024]{3,2,1,0:T(1,128)S(1)}, f32[2,6,1,1024]{3,2,1,0:T(1,128)S(1)}, u32[]{:S(2)}, u32[]{:S(2)}) collective-permute-start(f32[2,6,1,1024]{3,2,1,0:T(1,128)S(1)} %get-tuple-element.19), channel_id=1, source_target_pairs={{0,8},{8,16},{16,24},{24,32},{32,40},{40,48},{48,56},{56,64},{64,7... | collective-permute-start | bytes 147464 | tf_op jit(solution)/shard_map/ppermute | solution.py:22
  37.8 4.0 %collective-permute-start.10 = (f32[2,6,1,1024]{3,2,1,0:T(1,128)S(1)}, f32[2,6,1,1024]{3,2,1,0:T(1,128)S(1)}, u32[]{:S(2)}, u32[]{:S(2)}) collective-permute-start(f32[2,6,1,1024]{3,2,1,0:T(1,128)S(1)} %get-tuple-element.18), channel_id=1, source_target_pairs={{8,0},{16,8},{24,16},{32,24},{40,32},{48,40},{56,48},{64,56},{72,6... | collective-permute-start | bytes 147464 | tf_op jit(solution)/shard_map/ppermute | solution.py:22
  42.0 4.4 %collective-permute-done.5 = f32[2,2]{1,0:T(2,128)S(1)} collective-permute-done((f32[2,2]{1,0:T(2,128)S(1)}, f32[2,2]{1,0:T(2,128)S(1)}, u32[]{:S(2)}, u32[]{:S(2)}) %collective-permute-start.5) | collective-permute-done | bytes 48 | tf_op jit(solution)/shard_map/ppermute | solution.py:31
  46.5 3.2 %collective-permute-start.6 = (f32[2,2]{1,0:T(2,128)S(1)}, f32[2,2]{1,0:T(2,128)S(1)}, u32[]{:S(2)}, u32[]{:S(2)}) collective-permute-start(f32[2,2]{1,0:T(2,128)S(1)} %fusion.124), channel_id=1, source_target_pairs={{0,32},{8,40},{16,48},{24,56},{32,0},{40,8},{48,16},{56,24},{64,96... | collective-permute-start | bytes 56 | tf_op jit(solution)/shard_map/ppermute | solution.py:31
  49.7 4.4 %collective-permute-done.6 = f32[2,2]{1,0:T(2,128)S(1)} collective-permute-done((f32[2,2]{1,0:T(2,128)S(1)}, f32[2,2]{1,0:T(2,128)S(1)}, u32[]{:S(2)}, u32[]{:S(2)}) %collective-permute-start.6) | collective-permute-done | bytes 48 | tf_op jit(solution)/shard_map/ppermute | solution.py:31
  54.6 3.0 %collective-permute-done.7 = f32[2,2]{1,0:T(2,128)S(1)} collective-permute-done((f32[2,2]{1,0:T(2,128)S(1)}, f32[2,2]{1,0:T(2,128)S(1)}, u32[]{:S(2)}, u32[]{:S(2)}) %collective-permute-start.7) | collective-permute-done | bytes 48 | tf_op jit(solution)/shard_map/ppermute | solution.py:31
  57.6 1.1 %collective-permute-start.8 = (f32[2,2]{1,0:T(2,128)S(1)}, f32[2,2]{1,0:T(2,128)S(1)}, u32[]{:S(2)}, u32[]{:S(2)}) collective-permute-start(f32[2,2]{1,0:T(2,128)S(1)} %add.147), channel_id=1, source_target_pairs={{0,128},{8,136},{16,144},{24,152},{32,160},{40,168},{48,176},{56,1... | collective-permute-start | bytes 56 | tf_op jit(solution)/shard_map/ppermute | solution.py:31
  58.7 4.0 %collective-permute-done.8 = f32[2,2]{1,0:T(2,128)S(1)} collective-permute-done((f32[2,2]{1,0:T(2,128)S(1)}, f32[2,2]{1,0:T(2,128)S(1)}, u32[]{:S(2)}, u32[]{:S(2)}) %collective-permute-start.8) | collective-permute-done | bytes 48 | tf_op jit(solution)/shard_map/ppermute | solution.py:31
  62.7 0.6 fusion.120
  64.5 0.6 slice_add_fusion.3
  65.2 1.9 %collective-permute-start.11 = (f32[2,256]{1,0:T(2,128)S(1)}, f32[2,256]{1,0:T(2,128)S(1)}, u32[]{:S(2)}, u32[]{:S(2)}) collective-permute-start(f32[2,256]{1,0:T(2,128)S(1)} %slice.234), channel_id=1, source_target_pairs={{0,1},{1,2},{2,3},{3,4},{4,5},{5,6},{6,7},{8,9},{9,10},{10,11},{11... | collective-permute-start | bytes 6152 | tf_op jit(solution)/shard_map/ppermute | solution.py:22
  67.1 0.8 multiply_add_fusion.2
  68.0 0.6 slice_add_fusion.2
  68.6 1.5 %collective-permute-done.11 = f32[2,256]{1,0:T(2,128)S(1)} collective-permute-done((f32[2,256]{1,0:T(2,128)S(1)}, f32[2,256]{1,0:T(2,128)S(1)}, u32[]{:S(2)}, u32[]{:S(2)}) %collective-permute-start.11) | collective-permute-done | bytes 2080 | tf_op jit(solution)/shard_map/ppermute | solution.py:22
  70.1 2.4 %collective-permute-start.12 = (f32[2,256]{1,0:T(2,128)S(1)}, f32[2,256]{1,0:T(2,128)S(1)}, u32[]{:S(2)}, u32[]{:S(2)}) collective-permute-start(f32[2,256]{1,0:T(2,128)S(1)} %get-tuple-element.23), channel_id=1, source_target_pairs={{1,0},{2,1},{3,2},{4,3},{5,4},{6,5},{7,6},{9,8},{10,9},{11,10},{12... | collective-permute-start | bytes 6152 | tf_op jit(solution)/shard_map/ppermute | solution.py:22
  72.5 0.9 fusion.27
  73.6 0.9 fusion.33
  74.5 0.7 fusion.92
  75.3 0.6 pad_maximum_fusion.4.top_ref
  75.9 2.6 %shard_map.105 = f32[2,2,16,1024]{3,2,1,0:T(8,128)} custom-call(f32[2,2,16,1024]{3,2,1,0:T(8,128)} %get-tuple-element.8.u_ref, f32[2,5,1,1024]{3,2,1,0:T(1,128)} %pad_maximum_fusion.4.top_ref, f32[2,2,1,1024]{3,2,1,0:T(1,128)} %get-tuple-element.47.bot_ref, bf16[2,4,16,1024]{3,2,1,0:T(8,128)(2,1)} %k_ref.3, f32[8,1024]{1,0:T(8,128)} %broadcast_in_dim.2.keep_ref), custom_call_target="tpu_custom_call" | custom-call | tf_op jit(solution)/shard_map/pallas_call | solution.py:94
  78.5 1.2 %multiply_reduce_fusion.1 = (f32[2]{0:T(128)S(1)}, f32[2]{0:T(128)S(1)}) fusion(f32[2,2,16,1024]{3,2,1,0:T(8,128)} %shard_map.105, f32[1,2,16,1024]{3,2,1,0:T(8,128)S(1)} %fusion.33, f32[1,2,16,1024]{3,2,1,0:T(8,128)S(1)} %fusion.27, f32[2,2,16,1024]{3,2,1,0:T(8,128)S(1)} %get-tuple-element.9), kind=kLoop, calls=%fused_computation.48 | loop fusion | flops 524284 | bytes 786448 | tf_op jit(solution)/shard_map/reduce_sum | solution.py:205
  79.8 3.6 %collective-permute-done.13 = f32[2,2]{1,0:T(2,128)S(1)} collective-permute-done((f32[2,2]{1,0:T(2,128)S(1)}, f32[2,2]{1,0:T(2,128)S(1)}, u32[]{:S(2)}, u32[]{:S(2)}) %collective-permute-start.13) | collective-permute-done | bytes 48 | tf_op jit(solution)/shard_map/ppermute | solution.py:31
  83.5 4.4 %collective-permute-done.14 = f32[2,2]{1,0:T(2,128)S(1)} collective-permute-done((f32[2,2]{1,0:T(2,128)S(1)}, f32[2,2]{1,0:T(2,128)S(1)}, u32[]{:S(2)}, u32[]{:S(2)}) %collective-permute-start.14) | collective-permute-done | bytes 48 | tf_op jit(solution)/shard_map/ppermute | solution.py:31
  88.0 3.2 %collective-permute-start.15 = (f32[2,2]{1,0:T(2,128)S(1)}, f32[2,2]{1,0:T(2,128)S(1)}, u32[]{:S(2)}, u32[]{:S(2)}) collective-permute-start(f32[2,2]{1,0:T(2,128)S(1)} %fusion.123), channel_id=1, source_target_pairs={{0,32},{8,40},{16,48},{24,56},{32,0},{40,8},{48,16},{56,24},{64,96... | collective-permute-start | bytes 56 | tf_op jit(solution)/shard_map/ppermute | solution.py:31
  91.2 4.4 %collective-permute-done.15 = f32[2,2]{1,0:T(2,128)S(1)} collective-permute-done((f32[2,2]{1,0:T(2,128)S(1)}, f32[2,2]{1,0:T(2,128)S(1)}, u32[]{:S(2)}, u32[]{:S(2)}) %collective-permute-start.15) | collective-permute-done | bytes 48 | tf_op jit(solution)/shard_map/ppermute | solution.py:31
  96.1 3.0 %collective-permute-done.16 = f32[2,2]{1,0:T(2,128)S(1)} collective-permute-done((f32[2,2]{1,0:T(2,128)S(1)}, f32[2,2]{1,0:T(2,128)S(1)}, u32[]{:S(2)}, u32[]{:S(2)}) %collective-permute-start.16) | collective-permute-done | bytes 48 | tf_op jit(solution)/shard_map/ppermute | solution.py:31
  99.1 1.1 %collective-permute-start.17 = (f32[2,2]{1,0:T(2,128)S(1)}, f32[2,2]{1,0:T(2,128)S(1)}, u32[]{:S(2)}, u32[]{:S(2)}) collective-permute-start(f32[2,2]{1,0:T(2,128)S(1)} %add.165), channel_id=1, source_target_pairs={{0,128},{8,136},{16,144},{24,152},{32,160},{40,168},{48,176},{56,1... | collective-permute-start | bytes 56 | tf_op jit(solution)/shard_map/ppermute | solution.py:31
  100.2 4.0 %collective-permute-done.17 = f32[2,2]{1,0:T(2,128)S(1)} collective-permute-done((f32[2,2]{1,0:T(2,128)S(1)}, f32[2,2]{1,0:T(2,128)S(1)}, u32[]{:S(2)}, u32[]{:S(2)}) %collective-permute-start.17) | collective-permute-done | bytes 48 | tf_op jit(solution)/shard_map/ppermute | solution.py:31
  104.2 0.9 multiply_add_fusion
  (76 shorter events, 2.9 us)
Async XLA Ops:
  0.6 18.1 %copy-start = (f32[2,16,1024]{2,1,0:T(8,128)S(1)}, f32[2,16,1024]{2,1,0:T(8,128)}, u32[]{:S(2)}) copy-start(f32[2,16,1024]{2,1,0:T(8,128)} %param.12) | copy-start | bytes 393220
  0.6 6.4 %copy-start.1 = (f32[2,2,16,1024]{3,2,1,0:T(8,128)S(1)}, f32[2,2,16,1024]{3,2,1,0:T(8,128)}, u32[]{:S(2)}) copy-start(f32[2,2,16,1024]{3,2,1,0:T(8,128)} %u_ref.1) | copy-start | bytes 786436
  0.7 17.4 %copy-start.8 = (s32[2,2]{1,0:T(2,128)S(1)}, s32[2,2]{1,0:T(2,128)}, u32[]{:S(2)}) copy-start(s32[2,2]{1,0:T(2,128)} %param.17) | copy-start | bytes 52
  5.1 14.4 %collective-permute-start.2 = (f32[4,256]{1,0:T(4,128)S(1)}, f32[4,256]{1,0:T(4,128)S(1)}, u32[]{:S(2)}, u32[]{:S(2)}) collective-permute-start(f32[4,256]{1,0:T(4,128)S(1)} %pad_maximum_fusion.5), channel_id=1, source_target_pairs={{0,1},{1,2},{2,3},{3,4},{4,5},{5,6},{6,7},{8,9},{9,10},{10,11},{11... | collective-permute-start | bytes 12296 | tf_op jit(solution)/shard_map/ppermute | solution.py:22
  8.1 18.3 %collective-permute-start = (f32[2,5,1,1024]{3,2,1,0:T(1,128)S(1)}, f32[2,5,1,1024]{3,2,1,0:T(1,128)S(1)}, u32[]{:S(2)}, u32[]{:S(2)}) collective-permute-start(f32[2,5,1,1024]{3,2,1,0:T(1,128)S(1)} %pad_maximum_fusion.3), channel_id=1, source_target_pairs={{0,8},{8,16},{16,24},{24,32},{32,40},{40,48},{48,56},{56,64},{64,7... | collective-permute-start | bytes 122888 | tf_op jit(solution)/shard_map/ppermute | solution.py:22
  11.9 14.5 %collective-permute-start.1 = (f32[2,2,1,1024]{3,2,1,0:T(1,128)S(1)}, f32[2,2,1,1024]{3,2,1,0:T(1,128)S(1)}, u32[]{:S(2)}, u32[]{:S(2)}) collective-permute-start(f32[2,2,1,1024]{3,2,1,0:T(1,128)S(1)} %get-tuple-element.20), channel_id=1, source_target_pairs={{8,0},{16,8},{24,16},{32,24},{40,32},{48,40},{56,48},{64,56},{72,6... | collective-permute-start | bytes 49160 | tf_op jit(solution)/shard_map/ppermute | solution.py:22
  20.8 4.7 %collective-permute-start.3 = (f32[2,256]{1,0:T(2,128)S(1)}, f32[2,256]{1,0:T(2,128)S(1)}, u32[]{:S(2)}, u32[]{:S(2)}) collective-permute-start(f32[2,256]{1,0:T(2,128)S(1)} %get-tuple-element.27), channel_id=1, source_target_pairs={{1,0},{2,1},{3,2},{4,3},{5,4},{6,5},{7,6},{9,8},{10,9},{11,10},{12... | collective-permute-start | bytes 6152 | tf_op jit(solution)/shard_map/ppermute | solution.py:22
  26.4 0.7 copy-start.7
  26.4 0.7 copy-start.6
  27.1 3.8 %copy-start.5 = (f32[2,2,16,1024]{3,2,1,0:T(8,128)S(1)}, f32[2,2,16,1024]{3,2,1,0:T(8,128)}, u32[]{:S(2)}) copy-start(f32[2,2,16,1024]{3,2,1,0:T(8,128)} %param.10) | copy-start | bytes 786436
  29.7 1.3 %copy-start.2 = (f32[2,2,16,1024]{3,2,1,0:T(8,128)S(1)}, f32[2,2,16,1024]{3,2,1,0:T(8,128)}, u32[]{:S(2)}) copy-start(f32[2,2,16,1024]{3,2,1,0:T(8,128)} %u_ref.1) | copy-start | bytes 786436
  33.8 8.1 %collective-permute-start.4 = (f32[2,2]{1,0:T(2,128)S(1)}, f32[2,2]{1,0:T(2,128)S(1)}, u32[]{:S(2)}, u32[]{:S(2)}) collective-permute-start(f32[2,2]{1,0:T(2,128)S(1)} %pad_maximum_fusion.10), channel_id=1, source_target_pairs={{0,8},{8,0},{16,24},{24,16},{32,40},{40,32},{48,56},{56,48},{64,72... | collective-permute-start | bytes 56 | tf_op jit(solution)/shard_map/ppermute | solution.py:31
  33.9 40.6 %collective-permute-start.9 = (f32[2,6,1,1024]{3,2,1,0:T(1,128)S(1)}, f32[2,6,1,1024]{3,2,1,0:T(1,128)S(1)}, u32[]{:S(2)}, u32[]{:S(2)}) collective-permute-start(f32[2,6,1,1024]{3,2,1,0:T(1,128)S(1)} %get-tuple-element.19), channel_id=1, source_target_pairs={{0,8},{8,16},{16,24},{24,32},{32,40},{40,48},{48,56},{56,64},{64,7... | collective-permute-start | bytes 147464 | tf_op jit(solution)/shard_map/ppermute | solution.py:22
  37.8 36.7 %collective-permute-start.10 = (f32[2,6,1,1024]{3,2,1,0:T(1,128)S(1)}, f32[2,6,1,1024]{3,2,1,0:T(1,128)S(1)}, u32[]{:S(2)}, u32[]{:S(2)}) collective-permute-start(f32[2,6,1,1024]{3,2,1,0:T(1,128)S(1)} %get-tuple-element.18), channel_id=1, source_target_pairs={{8,0},{16,8},{24,16},{32,24},{40,32},{48,40},{56,48},{64,56},{72,6... | collective-permute-start | bytes 147464 | tf_op jit(solution)/shard_map/ppermute | solution.py:22
  41.9 4.6 %collective-permute-start.5 = (f32[2,2]{1,0:T(2,128)S(1)}, f32[2,2]{1,0:T(2,128)S(1)}, u32[]{:S(2)}, u32[]{:S(2)}) collective-permute-start(f32[2,2]{1,0:T(2,128)S(1)} %fusion.111), channel_id=1, source_target_pairs={{0,16},{8,24},{16,0},{24,8},{32,48},{40,56},{48,32},{56,40},{64,80... | collective-permute-start | bytes 56 | tf_op jit(solution)/shard_map/ppermute | solution.py:31
  46.5 7.6 %collective-permute-start.6 = (f32[2,2]{1,0:T(2,128)S(1)}, f32[2,2]{1,0:T(2,128)S(1)}, u32[]{:S(2)}, u32[]{:S(2)}) collective-permute-start(f32[2,2]{1,0:T(2,128)S(1)} %fusion.124), channel_id=1, source_target_pairs={{0,32},{8,40},{16,48},{24,56},{32,0},{40,8},{48,16},{56,24},{64,96... | collective-permute-start | bytes 56 | tf_op jit(solution)/shard_map/ppermute | solution.py:31
  54.0 3.6 %collective-permute-start.7 = (f32[2,2]{1,0:T(2,128)S(1)}, f32[2,2]{1,0:T(2,128)S(1)}, u32[]{:S(2)}, u32[]{:S(2)}) collective-permute-start(f32[2,2]{1,0:T(2,128)S(1)} %add.146), channel_id=1, source_target_pairs={{0,64},{8,72},{16,80},{24,88},{32,96},{40,104},{48,112},{56,120},{... | collective-permute-start | bytes 56 | tf_op jit(solution)/shard_map/ppermute | solution.py:31
  57.6 5.1 %collective-permute-start.8 = (f32[2,2]{1,0:T(2,128)S(1)}, f32[2,2]{1,0:T(2,128)S(1)}, u32[]{:S(2)}, u32[]{:S(2)}) collective-permute-start(f32[2,2]{1,0:T(2,128)S(1)} %add.147), channel_id=1, source_target_pairs={{0,128},{8,136},{16,144},{24,152},{32,160},{40,168},{48,176},{56,1... | collective-permute-start | bytes 56 | tf_op jit(solution)/shard_map/ppermute | solution.py:31
  65.2 4.9 %collective-permute-start.11 = (f32[2,256]{1,0:T(2,128)S(1)}, f32[2,256]{1,0:T(2,128)S(1)}, u32[]{:S(2)}, u32[]{:S(2)}) collective-permute-start(f32[2,256]{1,0:T(2,128)S(1)} %slice.234), channel_id=1, source_target_pairs={{0,1},{1,2},{2,3},{3,4},{4,5},{5,6},{6,7},{8,9},{9,10},{10,11},{11... | collective-permute-start | bytes 6152 | tf_op jit(solution)/shard_map/ppermute | solution.py:22
  68.0 7.3 %slice-start = ((f32[2,5,1,1024]{3,2,1,0:T(1,128)}), f32[2,3,1,1024]{3,2,1,0:T(1,128)S(1)}, s32[]{:S(2)}) async-start(f32[2,5,1,1024]{3,2,1,0:T(1,128)} %copy-done.6), calls=%async_computation | async-start | bytes 49152 | tf_op jit(solution)/shard_map/slice | solution.py:175
  70.1 3.5 %collective-permute-start.12 = (f32[2,256]{1,0:T(2,128)S(1)}, f32[2,256]{1,0:T(2,128)S(1)}, u32[]{:S(2)}, u32[]{:S(2)}) collective-permute-start(f32[2,256]{1,0:T(2,128)S(1)} %get-tuple-element.23), channel_id=1, source_target_pairs={{1,0},{2,1},{3,2},{4,3},{5,4},{6,5},{7,6},{9,8},{10,9},{11,10},{12... | collective-permute-start | bytes 6152 | tf_op jit(solution)/shard_map/ppermute | solution.py:22
  75.9 28.3 %copy-start.4 = (f32[2,2,16,1024]{3,2,1,0:T(8,128)S(1)}, f32[2,2,16,1024]{3,2,1,0:T(8,128)}, u32[]{:S(2)}) copy-start(f32[2,2,16,1024]{3,2,1,0:T(8,128)} %get-tuple-element.8.u_ref) | copy-start | bytes 786436
  78.5 25.7 %copy-start.3 = (f32[2,2,16,1024]{3,2,1,0:T(8,128)S(1)}, f32[2,2,16,1024]{3,2,1,0:T(8,128)}, u32[]{:S(2)}) copy-start(f32[2,2,16,1024]{3,2,1,0:T(8,128)} %shard_map.105) | copy-start | bytes 786436
  79.7 3.7 %collective-permute-start.13 = (f32[2,2]{1,0:T(2,128)S(1)}, f32[2,2]{1,0:T(2,128)S(1)}, u32[]{:S(2)}, u32[]{:S(2)}) collective-permute-start(f32[2,2]{1,0:T(2,128)S(1)} %pad_maximum_fusion.11), channel_id=1, source_target_pairs={{0,8},{8,0},{16,24},{24,16},{32,40},{40,32},{48,56},{56,48},{64,72... | collective-permute-start | bytes 56 | tf_op jit(solution)/shard_map/ppermute | solution.py:31
  83.4 4.6 %collective-permute-start.14 = (f32[2,2]{1,0:T(2,128)S(1)}, f32[2,2]{1,0:T(2,128)S(1)}, u32[]{:S(2)}, u32[]{:S(2)}) collective-permute-start(f32[2,2]{1,0:T(2,128)S(1)} %fusion.110), channel_id=1, source_target_pairs={{0,16},{8,24},{16,0},{24,8},{32,48},{40,56},{48,32},{56,40},{64,80... | collective-permute-start | bytes 56 | tf_op jit(solution)/shard_map/ppermute | solution.py:31
  88.0 7.6 %collective-permute-start.15 = (f32[2,2]{1,0:T(2,128)S(1)}, f32[2,2]{1,0:T(2,128)S(1)}, u32[]{:S(2)}, u32[]{:S(2)}) collective-permute-start(f32[2,2]{1,0:T(2,128)S(1)} %fusion.123), channel_id=1, source_target_pairs={{0,32},{8,40},{16,48},{24,56},{32,0},{40,8},{48,16},{56,24},{64,96... | collective-permute-start | bytes 56 | tf_op jit(solution)/shard_map/ppermute | solution.py:31
  95.5 3.6 %collective-permute-start.16 = (f32[2,2]{1,0:T(2,128)S(1)}, f32[2,2]{1,0:T(2,128)S(1)}, u32[]{:S(2)}, u32[]{:S(2)}) collective-permute-start(f32[2,2]{1,0:T(2,128)S(1)} %add.164), channel_id=1, source_target_pairs={{0,64},{8,72},{16,80},{24,88},{32,96},{40,104},{48,112},{56,120},{... | collective-permute-start | bytes 56 | tf_op jit(solution)/shard_map/ppermute | solution.py:31
  99.1 5.1 %collective-permute-start.17 = (f32[2,2]{1,0:T(2,128)S(1)}, f32[2,2]{1,0:T(2,128)S(1)}, u32[]{:S(2)}, u32[]{:S(2)}) collective-permute-start(f32[2,2]{1,0:T(2,128)S(1)} %add.165), channel_id=1, source_target_pairs={{0,128},{8,136},{16,144},{24,152},{32,160},{40,168},{48,176},{56,1... | collective-permute-start | bytes 56 | tf_op jit(solution)/shard_map/ppermute | solution.py:31
